TPU v7x, 32 devices: a whole 2x2x4 slice. The times are simulated.
32 devices in a mesh: dp: 4 (over y, x), fsdp: 8 (over z, core).
Axes of the slice: x: 2, y: 2, z: 4, core: 2. Of those that a mesh axis runs over, the one named last changes fastest.
Arguments:
- frames: bfloat16 [256, 1024, 512], P(('dp', 'fsdp')), may hold values from -6 to 6
- counts: int32 [256], P(('dp', 'fsdp')), may hold values from 64 to 1024, as said below
- cotangent: bfloat16 [256, 1024, 512], P(('dp', 'fsdp')), may hold values from -6 to 6
- master: float32 [1581056], P(('dp', 'fsdp'))
- momentum: float32 [1581056], P(('dp', 'fsdp')), may hold values from -48 to 48
- average: float32 [1581056], P(('dp', 'fsdp')), may hold values from -0.75 to 0.75
- disc_grads: float32 [1048576], P(('dp', 'fsdp'))
Outputs:
- block_out: bfloat16 [256, 1024, 512], P(('dp', 'fsdp'))
- input_grad: float32 [256, 1024, 512], P(('dp', 'fsdp'))
- grad_norm: float32 [], replicated
- new_master: float32 [1581056], P(('dp', 'fsdp'))
- new_momentum: float32 [1581056], P(('dp', 'fsdp'))
- new_average: float32 [1581056], P(('dp', 'fsdp'))
- master_copy: bfloat16 [1581056], P(('dp', 'fsdp'))
- average_copy: bfloat16 [1581056], P(('dp', 'fsdp'))
Inputs may be any that keep to these rules, and one draw needn't show every extreme that they name: `counts`: clip 0 has 1024 true frames and clip 1 has 64.
All inputs are finite; a program needn't handle non-finite values.
Results may differ from a plain program's by a relative error of at most 0.0014.
The roundings to bfloat16 on the way count: a program that leaves them out, or rounds other values in their place, can miss the bound.
Values may be sent and summed in bfloat16 or wider, within the bound.
No kernel may reach another device: no remote copies, remote signals or barrier semaphores. Data moves between devices by JAX's collectives and lax.ppermute only.
A program may use at most 320 MiB of HBM per device.

v0:
```python
import functools
import math

import jax
import jax.numpy as jnp
from jax import lax
from jax.experimental import pallas as pl
from jax.experimental.pallas import tpu as pltpu
from jax.sharding import PartitionSpec as P

F32 = jnp.float32
BF16 = jnp.bfloat16
TAPS = 7
HALF = TAPS // 2
PAD = 8
LANE = 128


def tdot(x, y):
    return lax.dot_general(x, y, (((0,), (0,)), ((), ())), preferred_element_type=F32)


def ntdot(x, y):
    return lax.dot_general(x, y, (((1,), (1,)), ((), ())), preferred_element_type=F32)


def block_kernel(length, width, hidden, rows, flat_rows):
    nblk = length // rows
    quads = width // LANE
    inv_w = 1.0 / width
    sqrt_half = math.sqrt(0.5)
    inv_sqrt_2pi = 1.0 / math.sqrt(2.0 * math.pi)

    def kernel(counts_ref, fr_ref, cot_ref, wrows_hbm, cw_ref, vec_ref, b1_ref,
               bo_ref, ig_ref, gflat_hbm, gcw_ref, gvec_ref, gb1_ref,
               xq, xhat_s, rstd_s, a_s, da_s, dq, gw1_s, gw2_s, flat_s, wb_s, w1_ref, w2_ref, sems):
        clip = pl.program_id(0)
        count = counts_ref[clip]

        @pl.when(clip == 0)
        def _weights():
            load = pltpu.make_async_copy(wrows_hbm.at[0:wb_s.shape[0], :], wb_s, sems.at[1])
            load.start()
            load.wait()
            wide = flat_s.at[0:wb_s.shape[0], :]
            wide[...] = wb_s[...].astype(F32)
            per1 = hidden // LANE
            per2 = width // LANE
            for j in range(per1):
                w1_ref[:, j * LANE:(j + 1) * LANE] = wide[pl.ds(j, width, stride=per1), :].astype(BF16)
            at = width * hidden // LANE
            for j in range(per2):
                w2_ref[:, j * LANE:(j + 1) * LANE] = wide[pl.ds(at + j, hidden, stride=per2), :].astype(BF16)

        @pl.when(clip == 0)
        def _init():
            gw1_s[...] = jnp.zeros_like(gw1_s)
            gw2_s[...] = jnp.zeros_like(gw2_s)
            gcw_ref[...] = jnp.zeros_like(gcw_ref)
            gvec_ref[...] = jnp.zeros_like(gvec_ref)
            gb1_ref[...] = jnp.zeros_like(gb1_ref)
            xq[0:PAD * quads, :] = jnp.zeros((PAD * quads, LANE), F32)
            xq[(PAD + length) * quads:, :] = jnp.zeros((PAD * quads, LANE), F32)
            dq[0:PAD * quads, :] = jnp.zeros((PAD * quads, LANE), F32)
            dq[(PAD + length) * quads:, :] = jnp.zeros((PAD * quads, LANE), F32)

        cw = cw_ref[...]
        conv_b = vec_ref[0:1, :]
        ln_g = vec_ref[1:2, :]
        ln_b = vec_ref[2:3, :]
        b_two = vec_ref[3:4, :]
        gamma = vec_ref[4:5, :]
        b_one = b1_ref[0:1, :]

        all_rows = lax.broadcasted_iota(jnp.int32, (length, 1), 0)
        xm_all = jnp.where(all_rows < count, fr_ref[0].astype(F32), 0.0)
        for q in range(quads):
            xq[pl.ds(PAD * quads + q, length, stride=quads), :] = xm_all[:, q * LANE:(q + 1) * LANE]

        def taps_of(buf, start):
            return jnp.concatenate(
                [buf[pl.ds(start * quads + q, rows, stride=quads), :] for q in range(quads)], axis=1)

        def fwd_block(b):
            r0 = pl.multiple_of(b * rows, rows)
            start = (PAD - HALF) * quads + r0 * quads
            conv = conv_b
            for k in range(TAPS):
                tap = jnp.concatenate(
                    [xq[pl.ds(start + k * quads + q, rows, stride=quads), :] for q in range(quads)], axis=1)
                conv = conv + cw[k:k + 1, :] * tap
            centre = jnp.sum(conv, axis=-1, keepdims=True) * inv_w
            shifted = conv - centre
            spread = jnp.sum(shifted * shifted, axis=-1, keepdims=True) * inv_w
            rstd = lax.rsqrt(spread + 1e-6)
            xhat = shifted * rstd
            xhat_s[pl.ds(r0, rows), :] = xhat
            rstd_s[pl.ds(r0, rows), :] = rstd
            a_s[pl.ds(r0, rows), :] = (xhat * ln_g + ln_b).astype(BF16)

        @pl.when(count > 0)
        def _first_block():
            fwd_block(0)

        bo_ref[...] = jnp.zeros_like(bo_ref)

        def chunk(c, carry):
            g_gamma, g_b2, g_b1 = carry
            r0 = pl.multiple_of(c * rows, rows)
            a = a_s[pl.ds(r0, rows), :]
            fwd_block(jnp.minimum(c + 1, nblk - 1))
            h1 = jnp.dot(a, w1_ref[...], preferred_element_type=F32) + b_one
            cdf = 0.5 * (1.0 + lax.erf(h1 * sqrt_half))
            hh = (h1 * cdf).astype(BF16)
            z = jnp.dot(hh, w2_ref[...], preferred_element_type=F32) + b_two
            live = (r0 + lax.broadcasted_iota(jnp.int32, (rows, 1), 0)) < count
            xin = fr_ref[0, pl.ds(r0, rows), :].astype(F32)
            bo_ref[0, pl.ds(r0, rows), :] = jnp.where(live, xin + gamma * z, 0.0).astype(BF16)
            dout = jnp.where(live, cot_ref[0, pl.ds(r0, rows), :].astype(F32), 0.0)
            g_gamma = g_gamma + jnp.sum(dout * z, axis=0, keepdims=True)
            dz = (gamma * dout).astype(BF16)
            g_b2 = g_b2 + jnp.sum(dz.astype(F32), axis=0, keepdims=True)
            gw2_s[...] += tdot(hh, dz)
            dhh = ntdot(dz, w2_ref[...])
            slope = cdf + h1 * (jnp.exp(-0.5 * (h1 * h1)) * inv_sqrt_2pi)
            dh1 = (dhh * slope).astype(BF16)
            g_b1 = g_b1 + jnp.sum(dh1.astype(F32), axis=0, keepdims=True)
            gw1_s[...] += tdot(a, dh1)
            da_s[pl.ds(r0, rows), :] = ntdot(dh1, w1_ref[...])
            return g_gamma, g_b2, g_b1

        nact = (count + rows - 1) // rows
        zero_d = jnp.zeros((1, width), F32)
        g_gamma, g_b2, g_b1 = lax.fori_loop(
            0, nact, chunk, (zero_d, zero_d, jnp.zeros((1, hidden), F32)))

        def dxm_block(b):
            r0 = b * rows
            base = PAD + r0 + HALF
            dxm = cw[0:1, :] * taps_of(dq, base)
            for k in range(1, TAPS):
                dxm = dxm + cw[k:k + 1, :] * taps_of(dq, base - k)
            live = (r0 + lax.broadcasted_iota(jnp.int32, (rows, 1), 0)) < count
            cot = cot_ref[0, r0:r0 + rows, :].astype(F32)
            ig_ref[0, r0:r0 + rows, :] = jnp.where(live, cot + dxm, 0.0)

        sums = [zero_d] * (3 + TAPS)
        for b in range(nblk):
            r0 = b * rows

            def _bwd_block(r0=r0):
                live = (r0 + lax.broadcasted_iota(jnp.int32, (rows, 1), 0)) < count
                da = jnp.where(live, da_s[r0:r0 + rows, :], 0.0)
                xhat = xhat_s[r0:r0 + rows, :]
                rstd = rstd_s[r0:r0 + rows, :]
                dn = da * ln_g
                m1 = jnp.sum(dn, axis=-1, keepdims=True) * inv_w
                m2 = jnp.sum(dn * xhat, axis=-1, keepdims=True) * inv_w
                dconv = jnp.where(live, rstd * (dn - m1 - xhat * m2), 0.0)
                for q in range(quads):
                    dq[pl.ds((PAD + r0) * quads + q, rows, stride=quads), :] = dconv[:, q * LANE:(q + 1) * LANE]
                part = [jnp.sum(dconv, axis=0, keepdims=True),
                        jnp.sum(da * xhat, axis=0, keepdims=True),
                        jnp.sum(da, axis=0, keepdims=True)]
                base = PAD + r0 - HALF
                for k in range(TAPS):
                    part.append(jnp.sum(dconv * taps_of(xq, base + k), axis=0, keepdims=True))
                return part

            active = r0 < count
            part = lax.cond(active, _bwd_block, lambda: [zero_d] * (3 + TAPS))

            @pl.when(jnp.logical_not(active))
            def _idle():
                dq[(PAD + r0) * quads:(PAD + r0 + rows) * quads, :] = jnp.zeros((rows * quads, LANE), F32)
                ig_ref[0, r0:r0 + rows, :] = jnp.zeros((rows, width), F32)

            sums = [s + p for s, p in zip(sums, part)]
            if b >= 1:
                @pl.when((b - 1) * rows < count)
                def _prev(b=b):
                    dxm_block(b - 1)

        @pl.when((nblk - 1) * rows < count)
        def _last():
            dxm_block(nblk - 1)

        gvec_ref[0:1, :] += sums[0]
        gvec_ref[1:2, :] += sums[1]
        gvec_ref[2:3, :] += sums[2]
        gvec_ref[3:4, :] += g_b2
        gvec_ref[4:5, :] += g_gamma
        for k in range(TAPS):
            gcw_ref[k:k + 1, :] += sums[3 + k]
        gb1_ref[0:1, :] += g_b1

        @pl.when(clip == pl.num_programs(0) - 1)
        def _flush():
            per1 = hidden // LANE
            per2 = width // LANE
            for j in range(per1):
                flat_s[pl.ds(j, width, stride=per1), :] = gw1_s[:, j * LANE:(j + 1) * LANE]
            at = width * hidden // LANE
            for j in range(per2):
                flat_s[pl.ds(at + j, hidden, stride=per2), :] = gw2_s[:, j * LANE:(j + 1) * LANE]
            at = 2 * at
            for q in range(per2):
                flat_s[pl.ds(at + q, TAPS, stride=per2), :] = gcw_ref[0:TAPS, q * LANE:(q + 1) * LANE]
            at = at + TAPS * per2
            for q in range(per2):
                flat_s[pl.ds(at + q, 5, stride=per2), :] = gvec_ref[0:5, q * LANE:(q + 1) * LANE]
            at = at + 5 * per2
            for j in range(per1):
                flat_s[at + j:at + j + 1, :] = gb1_ref[0:1, j * LANE:(j + 1) * LANE]
            at = at + per1
            flat_s[at:, :] = jnp.zeros((flat_rows - at, LANE), F32)
            out = pltpu.make_async_copy(flat_s, gflat_hbm, sems.at[0])
            out.start()
            out.wait()

    return kernel


def fused_block(frames, counts, cotangent, wrows, cw8, vec8, b1_8, flat_rows, rows=256):
    clips, length, width = frames.shape
    hidden = cw8.shape[1] * 3
    kernel = block_kernel(length, width, hidden, rows, flat_rows)
    clip_spec = pl.BlockSpec((1, length, width), lambda i, c: (i, 0, 0))
    fixed = lambda shape: pl.BlockSpec(shape, lambda i, c: (0, 0))
    grid_spec = pltpu.PrefetchScalarGridSpec(
        num_scalar_prefetch=1,
        grid=(clips,),
        in_specs=[clip_spec, clip_spec, pl.BlockSpec(memory_space=pl.ANY),
                  fixed((8, width)), fixed((8, width)), fixed((8, hidden))],
        out_specs=[clip_spec, clip_spec,
                   pl.BlockSpec(memory_space=pl.ANY),
                   fixed((8, width)), fixed((8, width)), fixed((8, hidden))],
        scratch_shapes=[
            pltpu.VMEM(((length + 2 * PAD) * (width // LANE), LANE), F32),
            pltpu.VMEM((length, width), F32),
            pltpu.VMEM((length, 1), F32),
            pltpu.VMEM((length, width), BF16),
            pltpu.VMEM((length, width), F32),
            pltpu.VMEM(((length + 2 * PAD) * (width // LANE), LANE), F32),
            pltpu.VMEM((width, hidden), F32),
            pltpu.VMEM((hidden, width), F32),
            pltpu.VMEM((flat_rows, LANE), F32),
            pltpu.VMEM((2 * width * hidden // LANE, LANE), BF16),
            pltpu.VMEM((width, hidden), BF16),
            pltpu.VMEM((hidden, width), BF16),
            pltpu.SemaphoreType.DMA((2,)),
        ],
    )
    flops = 12 * clips * length * width * hidden
    cost = pl.CostEstimate(flops=flops, transcendentals=2 * clips * length * hidden,
                           bytes_accessed=clips * length * width * 8 + 4 * width * hidden * 4)
    return pl.pallas_call(
        kernel,
        grid_spec=grid_spec,
        out_shape=[
            jax.ShapeDtypeStruct((clips, length, width), BF16),
            jax.ShapeDtypeStruct((clips, length, width), F32),
            jax.ShapeDtypeStruct((flat_rows, LANE), F32),
            jax.ShapeDtypeStruct((8, width), F32),
            jax.ShapeDtypeStruct((8, width), F32),
            jax.ShapeDtypeStruct((8, hidden), F32),
        ],
        compiler_params=pltpu.CompilerParams(
            dimension_semantics=("arbitrary",), vmem_limit_bytes=60 * 1024 * 1024),
        cost_estimate=cost,
    )(counts, frames, cotangent, wrows, cw8, vec8, b1_8)


def unpack(packed, width, hidden):
    shapes = [(width, hidden), (hidden, width), (TAPS, width), (width,), (width,), (width,), (width,), (width,), (hidden,)]
    pieces = []
    start_at = 0
    for shape in shapes:
        entries = 1
        for extent in shape:
            entries = entries * extent
        pieces.append(packed[start_at : start_at + entries].reshape(shape))
        start_at = start_at + entries
    return (tuple(pieces), start_at)


AXES = ("dp", "fsdp")
LANES = 128


def bit_order(mesh_sizes):
    dp_size, fsdp_size = mesh_sizes
    fsdp_bits = int(math.log2(fsdp_size))
    dp_bits = int(math.log2(dp_size))
    order = [0] + [fsdp_bits + b for b in range(dp_bits)] + list(range(1, fsdp_bits))
    return order, fsdp_bits + dp_bits


def swap_perm(devices, bit):
    return [(i, i ^ (1 << bit)) for i in range(devices)]


def split_orders(order):
    if len(order) < 3:
        return [order]
    other = [order[0], order[2], order[1]] + order[3:]
    return [order, other]


def tree_all_gather(shard, orders, nbits):
    me = lax.axis_index(AXES)
    devices = 1 << nbits
    rows = shard.shape[0]
    cuts = [rows * p // len(orders) for p in range(len(orders) + 1)]
    held = [shard[cuts[p]:cuts[p + 1]].reshape([1] * nbits + [-1, LANES]) for p in range(len(orders))]
    for step in range(nbits):
        for p, order in enumerate(orders):
            bit = order[step]
            other = lax.ppermute(held[p], AXES, swap_perm(devices, bit))
            upper = ((me >> bit) & 1) == 1
            held[p] = jnp.concatenate(
                [jnp.where(upper, other, held[p]), jnp.where(upper, held[p], other)], axis=nbits - 1 - bit)
    parts = [h.reshape(devices, -1, LANES) for h in held]
    return jnp.concatenate(parts, axis=1).reshape(devices * rows, LANES)


def tree_reduce_scatter(full, orders, nbits):
    me = lax.axis_index(AXES)
    devices = 1 << nbits
    rows = full.shape[0] // devices
    cuts = [rows * p // len(orders) for p in range(len(orders) + 1)]
    if rows % 8 == 0:
        cuts = [c // 8 * 8 for c in cuts]
    shaped = full.reshape([2] * nbits + [rows, LANES])
    held = [shaped[..., cuts[p]:cuts[p + 1], :] for p in range(len(orders))]
    held_bits = [[nbits - 1 - a for a in range(nbits)] for _ in orders]
    for step in range(nbits):
        for p, order in enumerate(orders):
            bit = order[step]
            axis = held_bits[p].index(bit)
            mine = (me >> bit) & 1
            keep = lax.dynamic_index_in_dim(held[p], mine, axis=axis, keepdims=False)
            send = lax.dynamic_index_in_dim(held[p], 1 - mine, axis=axis, keepdims=False)
            held[p] = keep + lax.ppermute(send, AXES, swap_perm(devices, bit))
            held_bits[p].pop(axis)
    return jnp.concatenate(held, axis=0)


def tree_all_sum(value, order, nbits):
    devices = 1 << nbits
    for bit in reversed(order):
        value = value + lax.ppermute(value, AXES, swap_perm(devices, bit))
    return value


def body(frames, counts, cotangent, master, momentum, average, disc_grads, mesh_sizes=None):
    order, nbits = bit_order(mesh_sizes)
    devices = 1 << nbits
    clips, length, width = frames.shape
    hidden = 3 * width
    rows = clips * length
    local = master.shape[0]
    flat_size = local * devices
    total_frames = jnp.float32(rows * devices)
    rounded = master.astype(BF16).reshape(local // LANES, LANES)
    packed_rows = tree_all_gather(rounded, [o[::-1] for o in split_orders(order)], nbits)
    weight_rows = 2 * width * hidden // LANES
    small_rows = -(-(TAPS * width + 5 * width + hidden) // LANES)
    small = packed_rows[weight_rows:weight_rows + small_rows].reshape(-1)
    conv_w = small[: TAPS * width].reshape(TAPS, width)
    at = TAPS * width
    conv_b, ln_g, ln_b, b_two, gamma = [small[at + i * width: at + (i + 1) * width] for i in range(5)]
    at = at + 5 * width
    b_one = small[at: at + hidden]
    cw8 = jnp.zeros((8, width), F32).at[:TAPS].set(conv_w.astype(F32))
    vec8 = jnp.concatenate(
        [jnp.stack([conv_b, ln_g, ln_b, b_two, gamma]).astype(F32), jnp.zeros((3, width), F32)])
    b1_8 = jnp.zeros((8, hidden), F32).at[0].set(b_one.astype(F32))
    shard_rows = local // LANES
    padded_rows = -(-shard_rows // 8) * 8
    aligned = padded_rows != shard_rows and (padded_rows - shard_rows) * (devices - 1) <= padded_rows
    block = padded_rows if aligned else shard_rows
    block_out, input_grad, grad_full, _, _, _ = fused_block(
        frames, counts, cotangent, packed_rows, cw8, vec8, b1_8, devices * block)
    grad_block = tree_reduce_scatter(grad_full, split_orders(order), nbits)
    if aligned:
        me = lax.axis_index(AXES)
        prev = lax.ppermute(grad_block, AXES, [(i, (i + 1) % devices) for i in range(devices)])
        both = jnp.concatenate([prev, grad_block])
        grad_shard = lax.dynamic_slice_in_dim(both, block - (block - shard_rows) * me, shard_rows, axis=0)
    else:
        grad_shard = grad_block
    disc_rows = jnp.sum((disc_grads * disc_grads).reshape(-1, LANES), axis=0, keepdims=True)
    own_rows = jnp.sum(grad_block * grad_block, axis=0, keepdims=True)
    squares = jnp.broadcast_to(own_rows + disc_rows, (8, LANES))
    squares = tree_all_sum(squares, order, nbits)
    grad_norm = jnp.sqrt(jnp.sum(squares[0]))
    grad_shard = grad_shard.reshape(-1)
    clipped = grad_shard * jnp.minimum(1.0, 20.0 * jnp.sqrt(total_frames) / (grad_norm + 1e-06))
    new_momentum = 0.9 * momentum + clipped
    new_master = master - (clipped + 0.9 * new_momentum) / jnp.sqrt(total_frames)
    new_average = 0.99 * average + 0.01 * new_master
    return (
        block_out,
        input_grad,
        grad_norm,
        new_master,
        new_momentum,
        new_average,
        new_master.astype(BF16),
        new_average.astype(BF16),
    )


def solution(mesh):
    clip_spec = P(("dp", "fsdp"), None, None)
    flat_spec = P(("dp", "fsdp"))
    mesh_sizes = (mesh.shape["dp"], mesh.shape["fsdp"])
    return jax.shard_map(
        functools.partial(body, mesh_sizes=mesh_sizes),
        mesh=mesh,
        in_specs=(clip_spec, flat_spec, clip_spec, flat_spec, flat_spec, flat_spec, flat_spec),
        out_specs=(clip_spec, clip_spec, P(), flat_spec, flat_spec, flat_spec, flat_spec, flat_spec),
        check_vma=False,
    )
```

profile of v0, /device:TPU:0, one launch (start us, length us, event | category | flops | bytes accessed | tf_op | source)
XLA Modules:
  0.0 271.6 jit_solution(13162937275487658146)
XLA Ops:
  1.6 4.1 %collective-permute-start = (bf16[1,1,1,1,1,193,128]{6,5,4,3,2,1,0:T(8,128)(2,1)S(1)}, bf16[1,1,1,1,1,193,128]{6,5,4,3,2,1,0:T(8,128)(2,1)S(1)}, u32[]{:S(2)}, u32[]{:S(2)}) collective-permute-start(bf16[1,1,1,1,1,193,128]{6,5,4,3,2,1,0:T(8,128)(2,1)S(1)} %get-tuple-element.71), channel_id=1, source_target_pairs={{0,4},{1,5},{2,6},{3,7},{4,0},{5,1},{6,2},{7,3},{8,12},{9,13},{10,... | collective-permute-start | bytes 148232 | tf_op jit(solution)/shard_map/ppermute | solution.py:319
  5.8 2.6 collective-permute-done
  8.4 2.5 collective-permute-done.5
  13.1 3.1 %collective-permute-done.1 = bf16[1,1,2,1,1,193,128]{6,5,4,3,2,1,0:T(8,128)(2,1)S(1)} collective-permute-done((bf16[1,1,2,1,1,193,128]{6,5,4,3,2,1,0:T(8,128)(2,1)S(1)}, bf16[1,1,2,1,1,193,128]{6,5,4,3,2,1,0:T(8,128)(2,1)S(1)}, u32[]{:S(2)}, u32[]{:S(2)}) %collective-permute-start.1) | collective-permute-done | bytes 98848 | tf_op jit(solution)/shard_map/ppermute | solution.py:319
  19.5 2.6 collective-permute-done.2
  23.8 2.2 collective-permute-done.7
  27.1 4.8 %collective-permute-done.3 = bf16[2,1,2,2,1,193,128]{6,5,4,3,2,1,0:T(8,128)(2,1)S(1)} collective-permute-done((bf16[2,1,2,2,1,193,128]{6,5,4,3,2,1,0:T(8,128)(2,1)S(1)}, bf16[2,1,2,2,1,193,128]{6,5,4,3,2,1,0:T(8,128)(2,1)S(1)}, u32[]{:S(2)}, u32[]{:S(2)}) %collective-permute-start.3) | collective-permute-done | bytes 395296 | tf_op jit(solution)/shard_map/ppermute | solution.py:319
  36.1 2.2 collective-permute-done.9
  42.9 2.7 reshape.141.wrows_hbm
  49.7 119.5 %shard_map.134 = (bf16[8,1024,512]{2,1,0:T(8,128)(2,1)}, f32[8,1024,512]{2,1,0:T(8,128)}, f32[12544,128]{1,0:T(8,128)}, f32[8,512]{1,0:T(8,128)}, f32[8,512]{1,0:T(8,128)}, /*index=5*/f32[8,1536]{1,0:T(8,128)}) custom-call(s32[8]{0:T(128)} %counts_ref.1, bf16[8,1024,512]{2,1,0:T(8,128)(2,1)} %fr_ref.1, bf16[8,1024,512]{2,1,0:T(8,128)(2,1)} %cot_ref.1, ...), custom_call_target="tpu_custom_call" | custom-call | flops 77309411328 | bytes 46137344 | tf_op jit(solution)/shard_map/pallas_call | solution.py:257
  169.2 2.3 slice.126
  184.7 15.8 %collective-permute-done.11 = f32[2,2,2,192,128]{4,3,2,1,0:T(8,128)} collective-permute-done((f32[2,2,2,192,128]{4,3,2,1,0:T(8,128)}, f32[2,2,2,192,128]{4,3,2,1,0:T(8,128)}, u32[]{:S(2)}, u32[]{:S(2)}) %collective-permute-start.11) | collective-permute-done | bytes 786464 | tf_op jit(solution)/shard_map/ppermute | solution.py:344
  202.7 3.3 %collective-permute-done.16 = f32[2,2,2,200,128]{4,3,2,1,0:T(8,128)} collective-permute-done((f32[2,2,2,200,128]{4,3,2,1,0:T(8,128)}, f32[2,2,2,200,128]{4,3,2,1,0:T(8,128)}, u32[]{:S(2)}, u32[]{:S(2)}) %collective-permute-start.16) | collective-permute-done | bytes 819232 | tf_op jit(solution)/shard_map/ppermute | solution.py:344
  209.2 4.5 %collective-permute-done.12 = f32[2,2,192,128]{3,2,1,0:T(8,128)} collective-permute-done((f32[2,2,192,128]{3,2,1,0:T(8,128)}, f32[2,2,192,128]{3,2,1,0:T(8,128)}, u32[]{:S(2)}, u32[]{:S(2)}) %collective-permute-start.12) | collective-permute-done | bytes 393248 | tf_op jit(solution)/shard_map/ppermute | solution.py:344
  214.9 2.6 collective-permute-done.17
  217.7 5.0 %collective-permute-done.13 = f32[2,192,128]{2,1,0:T(8,128)S(1)} collective-permute-done((f32[2,192,128]{2,1,0:T(8,128)S(1)}, f32[2,192,128]{2,1,0:T(8,128)S(1)}, u32[]{:S(2)}, u32[]{:S(2)}) %collective-permute-start.13) | collective-permute-done | bytes 196640 | tf_op jit(solution)/shard_map/ppermute | solution.py:344
  222.7 19.4 %collective-permute-start.14 = (f32[192,128]{1,0:T(8,128)S(1)}, f32[192,128]{1,0:T(8,128)S(1)}, u32[]{:S(2)}, u32[]{:S(2)}) collective-permute-start(f32[192,128]{1,0:T(8,128)S(1)} %dynamic-slice_bitcast_fusion.9), channel_id=1, source_target_pairs={{0,4},{1,5},{2,6},{3,7},{4,0},{5,1},{6,2},{7,3},{8,12},{9,13},{10,... | collective-permute-start | bytes 294920 | tf_op jit(solution)/shard_map/ppermute | solution.py:344
  242.2 3.8 %collective-permute-start.19 = (f32[200,128]{1,0:T(8,128)S(1)}, f32[200,128]{1,0:T(8,128)S(1)}, u32[]{:S(2)}, u32[]{:S(2)}) collective-permute-start(f32[200,128]{1,0:T(8,128)S(1)} %dynamic-slice_bitcast_fusion.8), channel_id=1, source_target_pairs={{0,4},{1,5},{2,6},{3,7},{4,0},{5,1},{6,2},{7,3},{8,12},{9,13},{10,... | collective-permute-start | bytes 307208 | tf_op jit(solution)/shard_map/ppermute | solution.py:344
  246.0 2.2 collective-permute-done.14
  248.2 2.5 collective-permute-done.19
  251.9 3.6 %collective-permute-done.20 = f32[8,128]{1,0:T(8,128)S(1)} collective-permute-done((f32[8,128]{1,0:T(8,128)S(1)}, f32[8,128]{1,0:T(8,128)S(1)}, u32[]{:S(2)}, u32[]{:S(2)}) %collective-permute-start.20) | collective-permute-done | bytes 4128 | tf_op jit(solution)/shard_map/ppermute | solution.py:352
  256.4 2.7 collective-permute-done.21
  259.6 3.0 %collective-permute-done.22 = f32[8,128]{1,0:T(8,128)S(1)} collective-permute-done((f32[8,128]{1,0:T(8,128)S(1)}, f32[8,128]{1,0:T(8,128)S(1)}, u32[]{:S(2)}, u32[]{:S(2)}) %collective-permute-start.22) | collective-permute-done | bytes 4128 | tf_op jit(solution)/shard_map/ppermute | solution.py:352
  263.3 3.0 %collective-permute-done.23 = f32[8,128]{1,0:T(8,128)S(1)} collective-permute-done((f32[8,128]{1,0:T(8,128)S(1)}, f32[8,128]{1,0:T(8,128)S(1)}, u32[]{:S(2)}, u32[]{:S(2)}) %collective-permute-start.23) | collective-permute-done | bytes 4128 | tf_op jit(solution)/shard_map/ppermute | solution.py:352
  (130 shorter events, 48.9 us)
Async XLA Ops:
  1.6 6.8 %collective-permute-start = (bf16[1,1,1,1,1,193,128]{6,5,4,3,2,1,0:T(8,128)(2,1)S(1)}, bf16[1,1,1,1,1,193,128]{6,5,4,3,2,1,0:T(8,128)(2,1)S(1)}, u32[]{:S(2)}, u32[]{:S(2)}) collective-permute-start(bf16[1,1,1,1,1,193,128]{6,5,4,3,2,1,0:T(8,128)(2,1)S(1)} %get-tuple-element.71), channel_id=1, source_target_pairs={{0,4},{1,5},{2,6},{3,7},{4,0},{5,1},{6,2},{7,3},{8,12},{9,13},{10,... | collective-permute-start | bytes 148232 | tf_op jit(solution)/shard_map/ppermute | solution.py:319
  5.7 5.2 %collective-permute-start.5 = (bf16[1,1,1,1,1,193,128]{6,5,4,3,2,1,0:T(8,128)(2,1)S(1)}, bf16[1,1,1,1,1,193,128]{6,5,4,3,2,1,0:T(8,128)(2,1)S(1)}, u32[]{:S(2)}, u32[]{:S(2)}) collective-permute-start(bf16[1,1,1,1,1,193,128]{6,5,4,3,2,1,0:T(8,128)(2,1)S(1)} %get-tuple-element.72), channel_id=1, source_target_pairs={{0,4},{1,5},{2,6},{3,7},{4,0},{5,1},{6,2},{7,3},{8,12},{9,13},{10,... | collective-permute-start | bytes 148232 | tf_op jit(solution)/shard_map/ppermute | solution.py:319
  11.0 5.3 %collective-permute-start.1 = (bf16[1,1,2,1,1,193,128]{6,5,4,3,2,1,0:T(8,128)(2,1)S(1)}, bf16[1,1,2,1,1,193,128]{6,5,4,3,2,1,0:T(8,128)(2,1)S(1)}, u32[]{:S(2)}, u32[]{:S(2)}) collective-permute-start(bf16[1,1,2,1,1,193,128]{6,5,4,3,2,1,0:T(8,128)(2,1)S(1)} %pad_maximum_fusion.10), channel_id=1, source_target_pairs={{0,2},{1,3},{2,0},{3,1},{4,6},{5,7},{6,4},{7,5},{8,10},{9,11},{10,... | collective-permute-start | bytes 296456 | tf_op jit(solution)/shard_map/ppermute | solution.py:319
  12.5 5.4 %collective-permute-start.6 = (bf16[1,1,2,1,1,193,128]{6,5,4,3,2,1,0:T(8,128)(2,1)S(1)}, bf16[1,1,2,1,1,193,128]{6,5,4,3,2,1,0:T(8,128)(2,1)S(1)}, u32[]{:S(2)}, u32[]{:S(2)}) collective-permute-start(bf16[1,1,2,1,1,193,128]{6,5,4,3,2,1,0:T(8,128)(2,1)S(1)} %pad_maximum_fusion.11), channel_id=1, source_target_pairs={{0,2},{1,3},{2,0},{3,1},{4,6},{5,7},{6,4},{7,5},{8,10},{9,11},{10,... | collective-permute-start | bytes 296456 | tf_op jit(solution)/shard_map/ppermute | solution.py:319
  16.3 5.8 %collective-permute-start.2 = (bf16[1,1,2,2,1,193,128]{6,5,4,3,2,1,0:T(8,128)(2,1)S(1)}, bf16[1,1,2,2,1,193,128]{6,5,4,3,2,1,0:T(8,128)(2,1)S(1)}, u32[]{:S(2)}, u32[]{:S(2)}) collective-permute-start(bf16[1,1,2,2,1,193,128]{6,5,4,3,2,1,0:T(8,128)(2,1)S(1)} %pad_maximum_fusion.7), channel_id=1, source_target_pairs={{0,16},{1,17},{2,18},{3,19},{4,20},{5,21},{6,22},{7,23},{8,24},{9,... | collective-permute-start | bytes 592904 | tf_op jit(solution)/shard_map/ppermute | solution.py:319
  18.0 8.0 %collective-permute-start.7 = (bf16[1,1,2,2,1,193,128]{6,5,4,3,2,1,0:T(8,128)(2,1)S(1)}, bf16[1,1,2,2,1,193,128]{6,5,4,3,2,1,0:T(8,128)(2,1)S(1)}, u32[]{:S(2)}, u32[]{:S(2)}) collective-permute-start(bf16[1,1,2,2,1,193,128]{6,5,4,3,2,1,0:T(8,128)(2,1)S(1)} %pad_maximum_fusion.8), channel_id=1, source_target_pairs={{0,8},{1,9},{2,10},{3,11},{4,12},{5,13},{6,14},{7,15},{8,0},{9,1},... | collective-permute-start | bytes 592904 | tf_op jit(solution)/shard_map/ppermute | solution.py:319
  22.2 9.7 %collective-permute-start.3 = (bf16[2,1,2,2,1,193,128]{6,5,4,3,2,1,0:T(8,128)(2,1)S(1)}, bf16[2,1,2,2,1,193,128]{6,5,4,3,2,1,0:T(8,128)(2,1)S(1)}, u32[]{:S(2)}, u32[]{:S(2)}) collective-permute-start(bf16[2,1,2,2,1,193,128]{6,5,4,3,2,1,0:T(8,128)(2,1)S(1)} %pad_maximum_fusion.5), channel_id=1, source_target_pairs={{0,8},{1,9},{2,10},{3,11},{4,12},{5,13},{6,14},{7,15},{8,0},{9,1},... | collective-permute-start | bytes 1185800 | tf_op jit(solution)/shard_map/ppermute | solution.py:319
  26.1 8.0 %collective-permute-start.8 = (bf16[1,2,2,2,1,193,128]{6,5,4,3,2,1,0:T(8,128)(2,1)S(1)}, bf16[1,2,2,2,1,193,128]{6,5,4,3,2,1,0:T(8,128)(2,1)S(1)}, u32[]{:S(2)}, u32[]{:S(2)}) collective-permute-start(bf16[1,2,2,2,1,193,128]{6,5,4,3,2,1,0:T(8,128)(2,1)S(1)} %pad_maximum_fusion.6), channel_id=1, source_target_pairs={{0,16},{1,17},{2,18},{3,19},{4,20},{5,21},{6,22},{7,23},{8,24},{9,... | collective-permute-start | bytes 1185800 | tf_op jit(solution)/shard_map/ppermute | solution.py:319
  33.6 2.5 collective-permute-start.4
  173.7 3.8 %collective-permute-start.10 = (f32[2,2,2,2,192,128]{5,4,3,2,1,0:T(8,128)}, f32[2,2,2,2,192,128]{5,4,3,2,1,0:T(8,128)}, u32[]{:S(2)}, u32[]{:S(2)}) collective-permute-start(f32[2,2,2,2,192,128]{5,4,3,2,1,0:T(8,128)} %dynamic-slice_bitcast_fusion.1), channel_id=1, source_target_pairs={{0,1},{1,0},{2,3},{3,2},{4,5},{5,4},{6,7},{7,6},{8,9},{9,8},{10,11... | collective-permute-start | bytes 4718600 | tf_op jit(solution)/shard_map/ppermute | solution.py:344
  175.8 5.2 %collective-permute-start.15 = (f32[2,2,2,2,200,128]{5,4,3,2,1,0:T(8,128)}, f32[2,2,2,2,200,128]{5,4,3,2,1,0:T(8,128)}, u32[]{:S(2)}, u32[]{:S(2)}) collective-permute-start(f32[2,2,2,2,200,128]{5,4,3,2,1,0:T(8,128)} %dynamic-slice_bitcast_fusion), channel_id=1, source_target_pairs={{0,1},{1,0},{2,3},{3,2},{4,5},{5,4},{6,7},{7,6},{8,9},{9,8},{10,11... | collective-permute-start | bytes 4915208 | tf_op jit(solution)/shard_map/ppermute | solution.py:344
  180.5 19.9 %collective-permute-start.11 = (f32[2,2,2,192,128]{4,3,2,1,0:T(8,128)}, f32[2,2,2,192,128]{4,3,2,1,0:T(8,128)}, u32[]{:S(2)}, u32[]{:S(2)}) collective-permute-start(f32[2,2,2,192,128]{4,3,2,1,0:T(8,128)} %dynamic-slice_bitcast_fusion.3), channel_id=1, source_target_pairs={{0,8},{1,9},{2,10},{3,11},{4,12},{5,13},{6,14},{7,15},{8,0},{9,1},... | collective-permute-start | bytes 2359304 | tf_op jit(solution)/shard_map/ppermute | solution.py:344
  184.7 21.3 %collective-permute-start.16 = (f32[2,2,2,200,128]{4,3,2,1,0:T(8,128)}, f32[2,2,2,200,128]{4,3,2,1,0:T(8,128)}, u32[]{:S(2)}, u32[]{:S(2)}) collective-permute-start(f32[2,2,2,200,128]{4,3,2,1,0:T(8,128)} %dynamic-slice_bitcast_fusion.2), channel_id=1, source_target_pairs={{0,16},{1,17},{2,18},{3,19},{4,20},{5,21},{6,22},{7,23},{8,24},{9,... | collective-permute-start | bytes 2457608 | tf_op jit(solution)/shard_map/ppermute | solution.py:344
  202.5 11.2 %collective-permute-start.12 = (f32[2,2,192,128]{3,2,1,0:T(8,128)}, f32[2,2,192,128]{3,2,1,0:T(8,128)}, u32[]{:S(2)}, u32[]{:S(2)}) collective-permute-start(f32[2,2,192,128]{3,2,1,0:T(8,128)} %dynamic-slice_bitcast_fusion.5), channel_id=1, source_target_pairs={{0,16},{1,17},{2,18},{3,19},{4,20},{5,21},{6,22},{7,23},{8,24},{9,... | collective-permute-start | bytes 1179656 | tf_op jit(solution)/shard_map/ppermute | solution.py:344
  207.3 10.2 %collective-permute-start.17 = (f32[2,2,200,128]{3,2,1,0:T(8,128)S(1)}, f32[2,2,200,128]{3,2,1,0:T(8,128)S(1)}, u32[]{:S(2)}, u32[]{:S(2)}) collective-permute-start(f32[2,2,200,128]{3,2,1,0:T(8,128)S(1)} %dynamic-slice_bitcast_fusion.4), channel_id=1, source_target_pairs={{0,8},{1,9},{2,10},{3,11},{4,12},{5,13},{6,14},{7,15},{8,0},{9,1},... | collective-permute-start | bytes 1228808 | tf_op jit(solution)/shard_map/ppermute | solution.py:344
  214.8 7.8 %collective-permute-start.13 = (f32[2,192,128]{2,1,0:T(8,128)S(1)}, f32[2,192,128]{2,1,0:T(8,128)S(1)}, u32[]{:S(2)}, u32[]{:S(2)}) collective-permute-start(f32[2,192,128]{2,1,0:T(8,128)S(1)} %dynamic-slice_bitcast_fusion.7), channel_id=1, source_target_pairs={{0,2},{1,3},{2,0},{3,1},{4,6},{5,7},{6,4},{7,5},{8,10},{9,11},{10,... | collective-permute-start | bytes 589832 | tf_op jit(solution)/shard_map/ppermute | solution.py:344
  217.6 24.6 %collective-permute-start.18 = (f32[2,200,128]{2,1,0:T(8,128)S(1)}, f32[2,200,128]{2,1,0:T(8,128)S(1)}, u32[]{:S(2)}, u32[]{:S(2)}) collective-permute-start(f32[2,200,128]{2,1,0:T(8,128)S(1)} %dynamic-slice_bitcast_fusion.6), channel_id=1, source_target_pairs={{0,2},{1,3},{2,0},{3,1},{4,6},{5,7},{6,4},{7,5},{8,10},{9,11},{10,... | collective-permute-start | bytes 614408 | tf_op jit(solution)/shard_map/ppermute | solution.py:344
  222.7 25.5 %collective-permute-start.14 = (f32[192,128]{1,0:T(8,128)S(1)}, f32[192,128]{1,0:T(8,128)S(1)}, u32[]{:S(2)}, u32[]{:S(2)}) collective-permute-start(f32[192,128]{1,0:T(8,128)S(1)} %dynamic-slice_bitcast_fusion.9), channel_id=1, source_target_pairs={{0,4},{1,5},{2,6},{3,7},{4,0},{5,1},{6,2},{7,3},{8,12},{9,13},{10,... | collective-permute-start | bytes 294920 | tf_op jit(solution)/shard_map/ppermute | solution.py:344
  242.2 8.5 %collective-permute-start.19 = (f32[200,128]{1,0:T(8,128)S(1)}, f32[200,128]{1,0:T(8,128)S(1)}, u32[]{:S(2)}, u32[]{:S(2)}) collective-permute-start(f32[200,128]{1,0:T(8,128)S(1)} %dynamic-slice_bitcast_fusion.8), channel_id=1, source_target_pairs={{0,4},{1,5},{2,6},{3,7},{4,0},{5,1},{6,2},{7,3},{8,12},{9,13},{10,... | collective-permute-start | bytes 307208 | tf_op jit(solution)/shard_map/ppermute | solution.py:344
  250.8 4.6 %collective-permute-start.20 = (f32[8,128]{1,0:T(8,128)S(1)}, f32[8,128]{1,0:T(8,128)S(1)}, u32[]{:S(2)}, u32[]{:S(2)}) collective-permute-start(f32[8,128]{1,0:T(8,128)S(1)} %broadcast_in_dim.2), channel_id=1, source_target_pairs={{0,4},{1,5},{2,6},{3,7},{4,0},{5,1},{6,2},{7,3},{8,12},{9,13},{10,... | collective-permute-start | bytes 12296 | tf_op jit(solution)/shard_map/ppermute | solution.py:352
  255.4 3.6 %collective-permute-start.21 = (f32[8,128]{1,0:T(8,128)S(1)}, f32[8,128]{1,0:T(8,128)S(1)}, u32[]{:S(2)}, u32[]{:S(2)}) collective-permute-start(f32[8,128]{1,0:T(8,128)S(1)} %broadcast_add_fusion), channel_id=1, source_target_pairs={{0,2},{1,3},{2,0},{3,1},{4,6},{5,7},{6,4},{7,5},{8,10},{9,11},{10,... | collective-permute-start | bytes 12296 | tf_op jit(solution)/shard_map/ppermute | solution.py:352
  256.4 12.4 %collective-permute-start.25 = (f32[392,128]{1,0:T(8,128)S(1)}, f32[392,128]{1,0:T(8,128)S(1)}, u32[]{:S(2)}, u32[]{:S(2)}) collective-permute-start(f32[392,128]{1,0:T(8,128)S(1)} %get-tuple-element.63), channel_id=1, source_target_pairs={{0,1},{1,2},{2,3},{3,4},{4,5},{5,6},{6,7},{7,8},{8,9},{9,10},{10,1... | collective-permute-start | bytes 602120 | tf_op jit(solution)/shard_map/ppermute | solution.py:388
  259.0 3.6 %collective-permute-start.22 = (f32[8,128]{1,0:T(8,128)S(1)}, f32[8,128]{1,0:T(8,128)S(1)}, u32[]{:S(2)}, u32[]{:S(2)}) collective-permute-start(f32[8,128]{1,0:T(8,128)S(1)} %fusion.5), channel_id=1, source_target_pairs={{0,16},{1,17},{2,18},{3,19},{4,20},{5,21},{6,22},{7,23},{8,24},{9,... | collective-permute-start | bytes 12296 | tf_op jit(solution)/shard_map/ppermute | solution.py:352
  262.6 3.6 %collective-permute-start.23 = (f32[8,128]{1,0:T(8,128)S(1)}, f32[8,128]{1,0:T(8,128)S(1)}, u32[]{:S(2)}, u32[]{:S(2)}) collective-permute-start(f32[8,128]{1,0:T(8,128)S(1)} %add.163), channel_id=1, source_target_pairs={{0,8},{1,9},{2,10},{3,11},{4,12},{5,13},{6,14},{7,15},{8,0},{9,1},... | collective-permute-start | bytes 12296 | tf_op jit(solution)/shard_map/ppermute | solution.py:352
  (15 other events, 221.4 us)
where the time goes:
time: 274 us; the launch traced here: 272 us
  Pallas kernels  119 us (43%)
  waiting for transfers between devices  71.8 us (26%)
  starting transfers between devices  40.5 us (15%)
  local copies, waits for them, and re-layouts  22.8 us (8%)
  other arithmetic  14.1 us (5%)
  between operations  2.9 us (1%)
    pallas_call x1, Pallas kernels, fused_block(): pl.pallas_call(kernel, grid_spec=grid_spec, out_shape=[jax.ShapeDtypeStru...  119 us
    ppermute x10, waiting for transfers between devices, tree_reduce_scatter(): held[p] = keep + lax.ppermute(send, AXES, swap_perm(devices, bit))  37.5 us
    ppermute x10, starting transfers between devices, tree_reduce_scatter(): held[p] = keep + lax.ppermute(send, AXES, swap_perm(devices, bit))  25.3 us
    ppermute x10, waiting for transfers between devices, tree_all_gather(): other = lax.ppermute(held[p], AXES, swap_perm(devices, bit))  20.9 us
    ppermute x5, waiting for transfers between devices, tree_all_sum(): value = value + lax.ppermute(value, AXES, swap_perm(devices, bit))  13.4 us
    ppermute x10, starting transfers between devices, tree_all_gather(): other = lax.ppermute(held[p], AXES, swap_perm(devices, bit))  12.1 us
    add x10, other arithmetic, tree_reduce_scatter(): held[p] = keep + lax.ppermute(send, AXES, swap_perm(devices, bit))  7.33 us
    squeeze x10, local copies, waits for them, and re-layouts, tree_reduce_scatter(): lax.dynamic_index_in_dim(held[p], 1 - mine, axis=axis, keepdims=False)  5.61 us
  transfers between devices with their start and end apart: 26, of which 22 were waited for; matrix products, arithmetic and copies ran while one was open for 6% of the time, Pallas kernels for 0%

commit v1 on v0

--- a/solution.py
+++ b/solution.py
@@ -312,6 +312,8 @@
     devices = 1 << nbits
     rows = shard.shape[0]
     cuts = [rows * p // len(orders) for p in range(len(orders) + 1)]
+    if rows >= 16 * len(orders):
+        cuts = [c // 16 * 16 for c in cuts[:-1]] + [rows]
     held = [shard[cuts[p]:cuts[p + 1]].reshape([1] * nbits + [-1, LANES]) for p in range(len(orders))]
     for step in range(nbits):
         for p, order in enumerate(orders):

time: 274 us -> 255 us (0.931)
  Pallas kernels: 119 us -> 104 us
  waiting for transfers between devices: 71.8 us -> 56.9 us
  starting transfers between devices: 40.5 us -> 53.6 us
    pallas_call x1, Pallas kernels: 119 us -> 104 us  [fused_block(): pl.pallas_call(kernel, grid_spec=grid_spec, out_shape=[jax.ShapeDtypeStru...]
    ppermute x10, starting transfers between devices: 25.3 us -> 36.7 us  [tree_reduce_scatter(): held[p] = keep + lax.ppermute(send, AXES, swap_perm(devices, bit))]
    ppermute x10, waiting for transfers between devices: 37.5 us -> 27.1 us  [tree_reduce_scatter(): held[p] = keep + lax.ppermute(send, AXES, swap_perm(devices, bit))]
    ppermute x10, waiting for transfers between devices: 20.9 us -> 15 us  [tree_all_gather(): other = lax.ppermute(held[p], AXES, swap_perm(devices, bit))]
    concatenate x4 -> x2, local copies, waits for them, and re-layouts: 5.43 us -> 1.84 us  [tree_all_gather(): jnp.concatenate([jnp.where(upper, other, held[p]), jnp.where(upper, held[...]
  transfers between devices with their start and end apart: 26 -> 26, of which waited for: 22 -> 21; matrix products, arithmetic and copies ran while one was open for 6% -> 7% of each run, Pallas kernels for 0% -> 0%
where the time goes in v1:
time: 255 us; the launch traced here: 253 us
  Pallas kernels  104 us (41%)
  waiting for transfers between devices  56.9 us (22%)
  starting transfers between devices  53.6 us (21%)
  local copies, waits for them, and re-layouts  20.1 us (8%)
  other arithmetic  16 us (6%)
  between operations  2.92 us (1%)
    pallas_call x1, Pallas kernels, fused_block(): pl.pallas_call(kernel, grid_spec=grid_spec, out_shape=[jax.ShapeDtypeStru...  104 us
    ppermute x10, starting transfers between devices, tree_reduce_scatter(): held[p] = keep + lax.ppermute(send, AXES, swap_perm(devices, bit))  36.7 us
    ppermute x10, waiting for transfers between devices, tree_reduce_scatter(): held[p] = keep + lax.ppermute(send, AXES, swap_perm(devices, bit))  27.1 us
    ppermute x10, waiting for transfers between devices, tree_all_gather(): other = lax.ppermute(held[p], AXES, swap_perm(devices, bit))  15 us
    ppermute x5, waiting for transfers between devices, tree_all_sum(): value = value + lax.ppermute(value, AXES, swap_perm(devices, bit))  14.8 us
    ppermute x10, starting transfers between devices, tree_all_gather(): other = lax.ppermute(held[p], AXES, swap_perm(devices, bit))  14.8 us
    add x10, other arithmetic, tree_reduce_scatter(): held[p] = keep + lax.ppermute(send, AXES, swap_perm(devices, bit))  7.33 us
    squeeze x10, local copies, waits for them, and re-layouts, tree_reduce_scatter(): lax.dynamic_index_in_dim(held[p], 1 - mine, axis=axis, keepdims=False)  5.6 us
  transfers between devices with their start and end apart: 26, of which 21 were waited for; matrix products, arithmetic and copies ran while one was open for 7% of the time, Pallas kernels for 0%

profile of v1, /device:TPU:0, one launch (start us, length us, event | category | flops | bytes accessed | tf_op | source)
XLA Modules:
  0.0 253.3 jit_solution(17520246573589549006)
XLA Ops:
  1.6 4.1 %collective-permute-start = (bf16[1,1,1,1,1,192,128]{6,5,4,3,2,1,0:T(8,128)(2,1)S(1)}, bf16[1,1,1,1,1,192,128]{6,5,4,3,2,1,0:T(8,128)(2,1)S(1)}, u32[]{:S(2)}, u32[]{:S(2)}) collective-permute-start(bf16[1,1,1,1,1,192,128]{6,5,4,3,2,1,0:T(8,128)(2,1)S(1)} %slice_bitcast_fusion.1), channel_id=1, source_target_pairs={{0,4},{1,5},{2,6},{3,7},{4,0},{5,1},{6,2},{7,3},{8,12},{9,13},{10,... | collective-permute-start | bytes 147464 | tf_op jit(solution)/shard_map/ppermute | solution.py:321
  5.8 2.5 collective-permute-done
  8.4 2.2 collective-permute-start.1
  17.3 2.5 collective-permute-done.2
  24.7 5.2 %collective-permute-done.3 = bf16[2,1,2,2,1,192,128]{6,5,4,3,2,1,0:T(8,128)(2,1)S(1)} collective-permute-done((bf16[2,1,2,2,1,192,128]{6,5,4,3,2,1,0:T(8,128)(2,1)S(1)}, bf16[2,1,2,2,1,192,128]{6,5,4,3,2,1,0:T(8,128)(2,1)S(1)}, u32[]{:S(2)}, u32[]{:S(2)}) %collective-permute-start.3) | collective-permute-done | bytes 393248 | tf_op jit(solution)/shard_map/ppermute | solution.py:321
  39.1 2.7 %reshape.131.wrows_hbm = bf16[12352,128]{1,0:T(8,128)(2,1)} reshape(bf16[32,386,128]{2,1,0:T(8,128)(2,1)S(1)} %copy.31) | data formatting | bytes 6324224 | tf_op jit(solution)/shard_map/reshape | solution.py:326
  45.9 103.7 %shard_map.134 = (bf16[8,1024,512]{2,1,0:T(8,128)(2,1)}, f32[8,1024,512]{2,1,0:T(8,128)}, f32[12544,128]{1,0:T(8,128)}, f32[8,512]{1,0:T(8,128)}, f32[8,512]{1,0:T(8,128)}, /*index=5*/f32[8,1536]{1,0:T(8,128)}) custom-call(s32[8]{0:T(128)} %counts_ref.1, bf16[8,1024,512]{2,1,0:T(8,128)(2,1)} %fr_ref.1, bf16[8,1024,512]{2,1,0:T(8,128)(2,1)} %cot_ref.1, ...), custom_call_target="tpu_custom_call" | custom-call | flops 77309411328 | bytes 46137344 | tf_op jit(solution)/shard_map/pallas_call | solution.py:257
  149.6 2.3 slice.104
  157.9 2.1 bitcast_add_fusion.1
  165.1 6.6 %collective-permute-start.16 = (f32[2,2,2,200,128]{4,3,2,1,0:T(8,128)}, f32[2,2,2,200,128]{4,3,2,1,0:T(8,128)}, u32[]{:S(2)}, u32[]{:S(2)}) collective-permute-start(f32[2,2,2,200,128]{4,3,2,1,0:T(8,128)} %dynamic-slice_bitcast_fusion.2), channel_id=1, source_target_pairs={{0,16},{1,17},{2,18},{3,19},{4,20},{5,21},{6,22},{7,23},{8,24},{9,... | collective-permute-start | bytes 2457608 | tf_op jit(solution)/shard_map/ppermute | solution.py:346
  171.7 9.2 %collective-permute-done.11 = f32[2,2,2,192,128]{4,3,2,1,0:T(8,128)} collective-permute-done((f32[2,2,2,192,128]{4,3,2,1,0:T(8,128)}, f32[2,2,2,192,128]{4,3,2,1,0:T(8,128)}, u32[]{:S(2)}, u32[]{:S(2)}) %collective-permute-start.11) | collective-permute-done | bytes 786464 | tf_op jit(solution)/shard_map/ppermute | solution.py:346
  182.9 5.2 %collective-permute-start.12 = (f32[2,2,192,128]{3,2,1,0:T(8,128)}, f32[2,2,192,128]{3,2,1,0:T(8,128)}, u32[]{:S(2)}, u32[]{:S(2)}) collective-permute-start(f32[2,2,192,128]{3,2,1,0:T(8,128)} %dynamic-slice_bitcast_fusion.5), channel_id=1, source_target_pairs={{0,16},{1,17},{2,18},{3,19},{4,20},{5,21},{6,22},{7,23},{8,24},{9,... | collective-permute-start | bytes 1179656 | tf_op jit(solution)/shard_map/ppermute | solution.py:346
  188.1 2.9 %collective-permute-done.16 = f32[2,2,2,200,128]{4,3,2,1,0:T(8,128)} collective-permute-done((f32[2,2,2,200,128]{4,3,2,1,0:T(8,128)}, f32[2,2,2,200,128]{4,3,2,1,0:T(8,128)}, u32[]{:S(2)}, u32[]{:S(2)}) %collective-permute-start.16) | collective-permute-done | bytes 819232 | tf_op jit(solution)/shard_map/ppermute | solution.py:346
  192.9 5.8 %collective-permute-done.12 = f32[2,2,192,128]{3,2,1,0:T(8,128)} collective-permute-done((f32[2,2,192,128]{3,2,1,0:T(8,128)}, f32[2,2,192,128]{3,2,1,0:T(8,128)}, u32[]{:S(2)}, u32[]{:S(2)}) %collective-permute-start.12) | collective-permute-done | bytes 393248 | tf_op jit(solution)/shard_map/ppermute | solution.py:346
  199.8 6.4 %collective-permute-start.13 = (f32[2,192,128]{2,1,0:T(8,128)S(1)}, f32[2,192,128]{2,1,0:T(8,128)S(1)}, u32[]{:S(2)}, u32[]{:S(2)}) collective-permute-start(f32[2,192,128]{2,1,0:T(8,128)S(1)} %dynamic-slice_bitcast_fusion.7), channel_id=1, source_target_pairs={{0,2},{1,3},{2,0},{3,1},{4,6},{5,7},{6,4},{7,5},{8,10},{9,11},{10,... | collective-permute-start | bytes 589832 | tf_op jit(solution)/shard_map/ppermute | solution.py:346
  206.3 2.6 %collective-permute-start.18 = (f32[2,200,128]{2,1,0:T(8,128)S(1)}, f32[2,200,128]{2,1,0:T(8,128)S(1)}, u32[]{:S(2)}, u32[]{:S(2)}) collective-permute-start(f32[2,200,128]{2,1,0:T(8,128)S(1)} %dynamic-slice_bitcast_fusion.6), channel_id=1, source_target_pairs={{0,2},{1,3},{2,0},{3,1},{4,6},{5,7},{6,4},{7,5},{8,10},{9,11},{10,... | collective-permute-start | bytes 614408 | tf_op jit(solution)/shard_map/ppermute | solution.py:346
  208.9 3.0 %collective-permute-done.13 = f32[2,192,128]{2,1,0:T(8,128)S(1)} collective-permute-done((f32[2,192,128]{2,1,0:T(8,128)S(1)}, f32[2,192,128]{2,1,0:T(8,128)S(1)}, u32[]{:S(2)}, u32[]{:S(2)}) %collective-permute-start.13) | collective-permute-done | bytes 196640 | tf_op jit(solution)/shard_map/ppermute | solution.py:346
  212.0 11.7 %collective-permute-start.14 = (f32[192,128]{1,0:T(8,128)S(1)}, f32[192,128]{1,0:T(8,128)S(1)}, u32[]{:S(2)}, u32[]{:S(2)}) collective-permute-start(f32[192,128]{1,0:T(8,128)S(1)} %dynamic-slice_bitcast_fusion.9), channel_id=1, source_target_pairs={{0,4},{1,5},{2,6},{3,7},{4,0},{5,1},{6,2},{7,3},{8,12},{9,13},{10,... | collective-permute-start | bytes 294920 | tf_op jit(solution)/shard_map/ppermute | solution.py:346
  223.7 3.8 %collective-permute-start.19 = (f32[200,128]{1,0:T(8,128)S(1)}, f32[200,128]{1,0:T(8,128)S(1)}, u32[]{:S(2)}, u32[]{:S(2)}) collective-permute-start(f32[200,128]{1,0:T(8,128)S(1)} %dynamic-slice_bitcast_fusion.8), channel_id=1, source_target_pairs={{0,4},{1,5},{2,6},{3,7},{4,0},{5,1},{6,2},{7,3},{8,12},{9,13},{10,... | collective-permute-start | bytes 307208 | tf_op jit(solution)/shard_map/ppermute | solution.py:346
  227.5 3.3 %collective-permute-done.14 = f32[192,128]{1,0:T(8,128)S(1)} collective-permute-done((f32[192,128]{1,0:T(8,128)S(1)}, f32[192,128]{1,0:T(8,128)S(1)}, u32[]{:S(2)}, u32[]{:S(2)}) %collective-permute-start.14) | collective-permute-done | bytes 98336 | tf_op jit(solution)/shard_map/ppermute | solution.py:346
  233.3 3.3 %collective-permute-done.20 = f32[8,128]{1,0:T(8,128)S(1)} collective-permute-done((f32[8,128]{1,0:T(8,128)S(1)}, f32[8,128]{1,0:T(8,128)S(1)}, u32[]{:S(2)}, u32[]{:S(2)}) %collective-permute-start.20) | collective-permute-done | bytes 4128 | tf_op jit(solution)/shard_map/ppermute | solution.py:354
  236.6 3.6 %collective-permute-done.21 = f32[8,128]{1,0:T(8,128)S(1)} collective-permute-done((f32[8,128]{1,0:T(8,128)S(1)}, f32[8,128]{1,0:T(8,128)S(1)}, u32[]{:S(2)}, u32[]{:S(2)}) %collective-permute-start.21) | collective-permute-done | bytes 4128 | tf_op jit(solution)/shard_map/ppermute | solution.py:354
  240.8 3.4 %collective-permute-done.22 = f32[8,128]{1,0:T(8,128)S(1)} collective-permute-done((f32[8,128]{1,0:T(8,128)S(1)}, f32[8,128]{1,0:T(8,128)S(1)}, u32[]{:S(2)}, u32[]{:S(2)}) %collective-permute-start.22) | collective-permute-done | bytes 4128 | tf_op jit(solution)/shard_map/ppermute | solution.py:354
  244.5 3.3 %collective-permute-done.23 = f32[8,128]{1,0:T(8,128)S(1)} collective-permute-done((f32[8,128]{1,0:T(8,128)S(1)}, f32[8,128]{1,0:T(8,128)S(1)}, u32[]{:S(2)}, u32[]{:S(2)}) %collective-permute-start.23) | collective-permute-done | bytes 4128 | tf_op jit(solution)/shard_map/ppermute | solution.py:354
  (130 shorter events, 49.0 us)
Async XLA Ops:
  1.6 6.7 %collective-permute-start = (bf16[1,1,1,1,1,192,128]{6,5,4,3,2,1,0:T(8,128)(2,1)S(1)}, bf16[1,1,1,1,1,192,128]{6,5,4,3,2,1,0:T(8,128)(2,1)S(1)}, u32[]{:S(2)}, u32[]{:S(2)}) collective-permute-start(bf16[1,1,1,1,1,192,128]{6,5,4,3,2,1,0:T(8,128)(2,1)S(1)} %slice_bitcast_fusion.1), channel_id=1, source_target_pairs={{0,4},{1,5},{2,6},{3,7},{4,0},{5,1},{6,2},{7,3},{8,12},{9,13},{10,... | collective-permute-start | bytes 147464 | tf_op jit(solution)/shard_map/ppermute | solution.py:321
  5.7 5.2 %collective-permute-start.5 = (bf16[1,1,1,1,1,194,128]{6,5,4,3,2,1,0:T(8,128)(2,1)S(1)}, bf16[1,1,1,1,1,194,128]{6,5,4,3,2,1,0:T(8,128)(2,1)S(1)}, u32[]{:S(2)}, u32[]{:S(2)}) collective-permute-start(bf16[1,1,1,1,1,194,128]{6,5,4,3,2,1,0:T(8,128)(2,1)S(1)} %slice_bitcast_fusion), channel_id=1, source_target_pairs={{0,4},{1,5},{2,6},{3,7},{4,0},{5,1},{6,2},{7,3},{8,12},{9,13},{10,... | collective-permute-start | bytes 149000 | tf_op jit(solution)/shard_map/ppermute | solution.py:321
  8.4 5.6 %collective-permute-start.1 = (bf16[1,1,2,1,1,192,128]{6,5,4,3,2,1,0:T(8,128)(2,1)S(1)}, bf16[1,1,2,1,1,192,128]{6,5,4,3,2,1,0:T(8,128)(2,1)S(1)}, u32[]{:S(2)}, u32[]{:S(2)}) collective-permute-start(bf16[1,1,2,1,1,192,128]{6,5,4,3,2,1,0:T(8,128)(2,1)S(1)} %pad_maximum_fusion.11), channel_id=1, source_target_pairs={{0,2},{1,3},{2,0},{3,1},{4,6},{5,7},{6,4},{7,5},{8,10},{9,11},{10,... | collective-permute-start | bytes 294920 | tf_op jit(solution)/shard_map/ppermute | solution.py:321
  10.9 4.7 %collective-permute-start.6 = (bf16[1,1,2,1,1,194,128]{6,5,4,3,2,1,0:T(8,128)(2,1)S(1)}, bf16[1,1,2,1,1,194,128]{6,5,4,3,2,1,0:T(8,128)(2,1)S(1)}, u32[]{:S(2)}, u32[]{:S(2)}) collective-permute-start(bf16[1,1,2,1,1,194,128]{6,5,4,3,2,1,0:T(8,128)(2,1)S(1)} %pad_maximum_fusion.10), channel_id=1, source_target_pairs={{0,2},{1,3},{2,0},{3,1},{4,6},{5,7},{6,4},{7,5},{8,10},{9,11},{10,... | collective-permute-start | bytes 297992 | tf_op jit(solution)/shard_map/ppermute | solution.py:321
  14.0 5.7 %collective-permute-start.2 = (bf16[1,1,2,2,1,192,128]{6,5,4,3,2,1,0:T(8,128)(2,1)S(1)}, bf16[1,1,2,2,1,192,128]{6,5,4,3,2,1,0:T(8,128)(2,1)S(1)}, u32[]{:S(2)}, u32[]{:S(2)}) collective-permute-start(bf16[1,1,2,2,1,192,128]{6,5,4,3,2,1,0:T(8,128)(2,1)S(1)} %pad_maximum_fusion.9), channel_id=1, source_target_pairs={{0,16},{1,17},{2,18},{3,19},{4,20},{5,21},{6,22},{7,23},{8,24},{9,... | collective-permute-start | bytes 589832 | tf_op jit(solution)/shard_map/ppermute | solution.py:321
  15.7 7.2 %collective-permute-start.7 = (bf16[1,1,2,2,1,194,128]{6,5,4,3,2,1,0:T(8,128)(2,1)S(1)}, bf16[1,1,2,2,1,194,128]{6,5,4,3,2,1,0:T(8,128)(2,1)S(1)}, u32[]{:S(2)}, u32[]{:S(2)}) collective-permute-start(bf16[1,1,2,2,1,194,128]{6,5,4,3,2,1,0:T(8,128)(2,1)S(1)} %pad_maximum_fusion.7), channel_id=1, source_target_pairs={{0,8},{1,9},{2,10},{3,11},{4,12},{5,13},{6,14},{7,15},{8,0},{9,1},... | collective-permute-start | bytes 595976 | tf_op jit(solution)/shard_map/ppermute | solution.py:321
  19.8 10.2 %collective-permute-start.3 = (bf16[2,1,2,2,1,192,128]{6,5,4,3,2,1,0:T(8,128)(2,1)S(1)}, bf16[2,1,2,2,1,192,128]{6,5,4,3,2,1,0:T(8,128)(2,1)S(1)}, u32[]{:S(2)}, u32[]{:S(2)}) collective-permute-start(bf16[2,1,2,2,1,192,128]{6,5,4,3,2,1,0:T(8,128)(2,1)S(1)} %pad_maximum_fusion.6), channel_id=1, source_target_pairs={{0,8},{1,9},{2,10},{3,11},{4,12},{5,13},{6,14},{7,15},{8,0},{9,1},... | collective-permute-start | bytes 1179656 | tf_op jit(solution)/shard_map/ppermute | solution.py:321
  23.0 8.0 %collective-permute-start.8 = (bf16[1,2,2,2,1,194,128]{6,5,4,3,2,1,0:T(8,128)(2,1)S(1)}, bf16[1,2,2,2,1,194,128]{6,5,4,3,2,1,0:T(8,128)(2,1)S(1)}, u32[]{:S(2)}, u32[]{:S(2)}) collective-permute-start(bf16[1,2,2,2,1,194,128]{6,5,4,3,2,1,0:T(8,128)(2,1)S(1)} %pad_maximum_fusion.5), channel_id=1, source_target_pairs={{0,16},{1,17},{2,18},{3,19},{4,20},{5,21},{6,22},{7,23},{8,24},{9,... | collective-permute-start | bytes 1191944 | tf_op jit(solution)/shard_map/ppermute | solution.py:321
  31.8 4.2 %collective-permute-start.9 = (bf16[2,2,2,2,1,194,128]{6,3,5,4,2,1,0:T(2,128)(2,1)S(1)}, bf16[2,2,2,2,1,194,128]{6,3,5,4,2,1,0:T(2,128)(2,1)S(1)}, u32[]{:S(2)}, u32[]{:S(2)}) collective-permute-start(bf16[2,2,2,2,1,194,128]{6,3,5,4,2,1,0:T(2,128)(2,1)S(1)} %copy.26), channel_id=1, source_target_pairs={{0,1},{1,0},{2,3},{3,2},{4,5},{5,4},{6,7},{7,6},{8,9},{9,8},{10,11... | collective-permute-start | bytes 2383880 | tf_op jit(solution)/shard_map/ppermute | solution.py:321
  154.1 3.8 %collective-permute-start.10 = (f32[2,2,2,2,192,128]{5,4,3,2,1,0:T(8,128)}, f32[2,2,2,2,192,128]{5,4,3,2,1,0:T(8,128)}, u32[]{:S(2)}, u32[]{:S(2)}) collective-permute-start(f32[2,2,2,2,192,128]{5,4,3,2,1,0:T(8,128)} %dynamic-slice_bitcast_fusion.1), channel_id=1, source_target_pairs={{0,1},{1,0},{2,3},{3,2},{4,5},{5,4},{6,7},{7,6},{8,9},{9,8},{10,11... | collective-permute-start | bytes 4718600 | tf_op jit(solution)/shard_map/ppermute | solution.py:346
  156.2 5.2 %collective-permute-start.15 = (f32[2,2,2,2,200,128]{5,4,3,2,1,0:T(8,128)}, f32[2,2,2,2,200,128]{5,4,3,2,1,0:T(8,128)}, u32[]{:S(2)}, u32[]{:S(2)}) collective-permute-start(f32[2,2,2,2,200,128]{5,4,3,2,1,0:T(8,128)} %dynamic-slice_bitcast_fusion), channel_id=1, source_target_pairs={{0,1},{1,0},{2,3},{3,2},{4,5},{5,4},{6,7},{7,6},{8,9},{9,8},{10,11... | collective-permute-start | bytes 4915208 | tf_op jit(solution)/shard_map/ppermute | solution.py:346
  160.9 19.9 %collective-permute-start.11 = (f32[2,2,2,192,128]{4,3,2,1,0:T(8,128)}, f32[2,2,2,192,128]{4,3,2,1,0:T(8,128)}, u32[]{:S(2)}, u32[]{:S(2)}) collective-permute-start(f32[2,2,2,192,128]{4,3,2,1,0:T(8,128)} %dynamic-slice_bitcast_fusion.3), channel_id=1, source_target_pairs={{0,8},{1,9},{2,10},{3,11},{4,12},{5,13},{6,14},{7,15},{8,0},{9,1},... | collective-permute-start | bytes 2359304 | tf_op jit(solution)/shard_map/ppermute | solution.py:346
  165.1 26.0 %collective-permute-start.16 = (f32[2,2,2,200,128]{4,3,2,1,0:T(8,128)}, f32[2,2,2,200,128]{4,3,2,1,0:T(8,128)}, u32[]{:S(2)}, u32[]{:S(2)}) collective-permute-start(f32[2,2,2,200,128]{4,3,2,1,0:T(8,128)} %dynamic-slice_bitcast_fusion.2), channel_id=1, source_target_pairs={{0,16},{1,17},{2,18},{3,19},{4,20},{5,21},{6,22},{7,23},{8,24},{9,... | collective-permute-start | bytes 2457608 | tf_op jit(solution)/shard_map/ppermute | solution.py:346
  182.9 15.8 %collective-permute-start.12 = (f32[2,2,192,128]{3,2,1,0:T(8,128)}, f32[2,2,192,128]{3,2,1,0:T(8,128)}, u32[]{:S(2)}, u32[]{:S(2)}) collective-permute-start(f32[2,2,192,128]{3,2,1,0:T(8,128)} %dynamic-slice_bitcast_fusion.5), channel_id=1, source_target_pairs={{0,16},{1,17},{2,18},{3,19},{4,20},{5,21},{6,22},{7,23},{8,24},{9,... | collective-permute-start | bytes 1179656 | tf_op jit(solution)/shard_map/ppermute | solution.py:346
  192.4 13.7 %collective-permute-start.17 = (f32[2,2,200,128]{3,2,1,0:T(8,128)S(1)}, f32[2,2,200,128]{3,2,1,0:T(8,128)S(1)}, u32[]{:S(2)}, u32[]{:S(2)}) collective-permute-start(f32[2,2,200,128]{3,2,1,0:T(8,128)S(1)} %dynamic-slice_bitcast_fusion.4), channel_id=1, source_target_pairs={{0,8},{1,9},{2,10},{3,11},{4,12},{5,13},{6,14},{7,15},{8,0},{9,1},... | collective-permute-start | bytes 1228808 | tf_op jit(solution)/shard_map/ppermute | solution.py:346
  199.8 12.1 %collective-permute-start.13 = (f32[2,192,128]{2,1,0:T(8,128)S(1)}, f32[2,192,128]{2,1,0:T(8,128)S(1)}, u32[]{:S(2)}, u32[]{:S(2)}) collective-permute-start(f32[2,192,128]{2,1,0:T(8,128)S(1)} %dynamic-slice_bitcast_fusion.7), channel_id=1, source_target_pairs={{0,2},{1,3},{2,0},{3,1},{4,6},{5,7},{6,4},{7,5},{8,10},{9,11},{10,... | collective-permute-start | bytes 589832 | tf_op jit(solution)/shard_map/ppermute | solution.py:346
  206.3 17.4 %collective-permute-start.18 = (f32[2,200,128]{2,1,0:T(8,128)S(1)}, f32[2,200,128]{2,1,0:T(8,128)S(1)}, u32[]{:S(2)}, u32[]{:S(2)}) collective-permute-start(f32[2,200,128]{2,1,0:T(8,128)S(1)} %dynamic-slice_bitcast_fusion.6), channel_id=1, source_target_pairs={{0,2},{1,3},{2,0},{3,1},{4,6},{5,7},{6,4},{7,5},{8,10},{9,11},{10,... | collective-permute-start | bytes 614408 | tf_op jit(solution)/shard_map/ppermute | solution.py:346
  212.0 18.8 %collective-permute-start.14 = (f32[192,128]{1,0:T(8,128)S(1)}, f32[192,128]{1,0:T(8,128)S(1)}, u32[]{:S(2)}, u32[]{:S(2)}) collective-permute-start(f32[192,128]{1,0:T(8,128)S(1)} %dynamic-slice_bitcast_fusion.9), channel_id=1, source_target_pairs={{0,4},{1,5},{2,6},{3,7},{4,0},{5,1},{6,2},{7,3},{8,12},{9,13},{10,... | collective-permute-start | bytes 294920 | tf_op jit(solution)/shard_map/ppermute | solution.py:346
  223.7 8.2 %collective-permute-start.19 = (f32[200,128]{1,0:T(8,128)S(1)}, f32[200,128]{1,0:T(8,128)S(1)}, u32[]{:S(2)}, u32[]{:S(2)}) collective-permute-start(f32[200,128]{1,0:T(8,128)S(1)} %dynamic-slice_bitcast_fusion.8), channel_id=1, source_target_pairs={{0,4},{1,5},{2,6},{3,7},{4,0},{5,1},{6,2},{7,3},{8,12},{9,13},{10,... | collective-permute-start | bytes 307208 | tf_op jit(solution)/shard_map/ppermute | solution.py:346
  232.0 4.6 %collective-permute-start.20 = (f32[8,128]{1,0:T(8,128)S(1)}, f32[8,128]{1,0:T(8,128)S(1)}, u32[]{:S(2)}, u32[]{:S(2)}) collective-permute-start(f32[8,128]{1,0:T(8,128)S(1)} %broadcast_in_dim.2), channel_id=1, source_target_pairs={{0,4},{1,5},{2,6},{3,7},{4,0},{5,1},{6,2},{7,3},{8,12},{9,13},{10,... | collective-permute-start | bytes 12296 | tf_op jit(solution)/shard_map/ppermute | solution.py:354
  236.6 3.6 %collective-permute-start.21 = (f32[8,128]{1,0:T(8,128)S(1)}, f32[8,128]{1,0:T(8,128)S(1)}, u32[]{:S(2)}, u32[]{:S(2)}) collective-permute-start(f32[8,128]{1,0:T(8,128)S(1)} %broadcast_add_fusion), channel_id=1, source_target_pairs={{0,2},{1,3},{2,0},{3,1},{4,6},{5,7},{6,4},{7,5},{8,10},{9,11},{10,... | collective-permute-start | bytes 12296 | tf_op jit(solution)/shard_map/ppermute | solution.py:354
  236.6 13.7 %collective-permute-start.25 = (f32[392,128]{1,0:T(8,128)S(1)}, f32[392,128]{1,0:T(8,128)S(1)}, u32[]{:S(2)}, u32[]{:S(2)}) collective-permute-start(f32[392,128]{1,0:T(8,128)S(1)} %get-tuple-element.61), channel_id=1, source_target_pairs={{0,1},{1,2},{2,3},{3,4},{4,5},{5,6},{6,7},{7,8},{8,9},{9,10},{10,1... | collective-permute-start | bytes 602120 | tf_op jit(solution)/shard_map/ppermute | solution.py:390
  240.2 4.0 %collective-permute-start.22 = (f32[8,128]{1,0:T(8,128)S(1)}, f32[8,128]{1,0:T(8,128)S(1)}, u32[]{:S(2)}, u32[]{:S(2)}) collective-permute-start(f32[8,128]{1,0:T(8,128)S(1)} %fusion.5), channel_id=1, source_target_pairs={{0,16},{1,17},{2,18},{3,19},{4,20},{5,21},{6,22},{7,23},{8,24},{9,... | collective-permute-start | bytes 12296 | tf_op jit(solution)/shard_map/ppermute | solution.py:354
  244.2 3.6 %collective-permute-start.23 = (f32[8,128]{1,0:T(8,128)S(1)}, f32[8,128]{1,0:T(8,128)S(1)}, u32[]{:S(2)}, u32[]{:S(2)}) collective-permute-start(f32[8,128]{1,0:T(8,128)S(1)} %add.163), channel_id=1, source_target_pairs={{0,8},{1,9},{2,10},{3,11},{4,12},{5,13},{6,14},{7,15},{8,0},{9,1},... | collective-permute-start | bytes 12296 | tf_op jit(solution)/shard_map/ppermute | solution.py:354
  (15 other events, 213.2 us)

commit v2 on v1

--- a/solution.py
+++ b/solution.py
@@ -24,16 +24,19 @@
     return lax.dot_general(x, y, (((1,), (1,)), ((), ())), preferred_element_type=F32)
 
 
-def block_kernel(length, width, hidden, rows, flat_rows):
+def block_kernel(length, width, hidden, rows, flat_rows, split):
     nblk = length // rows
     quads = width // LANE
     inv_w = 1.0 / width
     sqrt_half = math.sqrt(0.5)
     inv_sqrt_2pi = 1.0 / math.sqrt(2.0 * math.pi)
 
-    def kernel(counts_ref, fr_ref, cot_ref, wrows_hbm, cw_ref, vec_ref, b1_ref,
-               bo_ref, ig_ref, gflat_hbm, gcw_ref, gvec_ref, gb1_ref,
-               xq, xhat_s, rstd_s, a_s, da_s, dq, gw1_s, gw2_s, flat_s, wb_s, w1_ref, w2_ref, sems):
+    def kernel(counts_ref, bit_ref, fr_ref, cot_ref, wrows_hbm, cw_ref, vec_ref, b1_ref, *refs):
+        n_out = 2 if split else 1
+        bo_ref, ig_ref = refs[0:2]
+        g_refs = refs[2:2 + n_out]
+        gcw_ref, gvec_ref, gb1_ref = refs[2 + n_out:5 + n_out]
+        (xq, xhat_s, rstd_s, a_s, da_s, dq, gw1_s, gw2_s, flat_s, wb_s, w1_ref, w2_ref, sems) = refs[5 + n_out:]
         clip = pl.program_id(0)
         count = counts_ref[clip]
 
@@ -214,27 +217,49 @@
                 flat_s[at + j:at + j + 1, :] = gb1_ref[0:1, j * LANE:(j + 1) * LANE]
             at = at + per1
             flat_s[at:, :] = jnp.zeros((flat_rows - at, LANE), F32)
-            out = pltpu.make_async_copy(flat_s, gflat_hbm, sems.at[0])
-            out.start()
-            out.wait()
+            if split:
+                block, cuts = split
+                mine = bit_ref[0]
+                copies = []
+                for s in range(flat_rows // block):
+                    side = lax.rem(mine + s % 2, 2)
+                    for p in range(len(cuts) - 1):
+                        copies.append(pltpu.make_async_copy(
+                            flat_s.at[pl.ds(s * block + cuts[p], cuts[p + 1] - cuts[p]), :],
+                            g_refs[p].at[side, s // 2], sems.at[2 + len(copies)]))
+                for cp in copies:
+                    cp.start()
+                for cp in copies:
+                    cp.wait()
+            else:
+                out = pltpu.make_async_copy(flat_s, g_refs[0], sems.at[0])
+                out.start()
+                out.wait()
 
     return kernel
 
 
-def fused_block(frames, counts, cotangent, wrows, cw8, vec8, b1_8, flat_rows, rows=256):
+def fused_block(frames, counts, cotangent, wrows, cw8, vec8, b1_8, flat_rows, my_bit, split=None, rows=256):
     clips, length, width = frames.shape
     hidden = cw8.shape[1] * 3
-    kernel = block_kernel(length, width, hidden, rows, flat_rows)
-    clip_spec = pl.BlockSpec((1, length, width), lambda i, c: (i, 0, 0))
-    fixed = lambda shape: pl.BlockSpec(shape, lambda i, c: (0, 0))
+    kernel = block_kernel(length, width, hidden, rows, flat_rows, split)
+    if split:
+        block, cuts = split
+        half = flat_rows // block // 2
+        grad_shapes = [(2, half, cuts[p + 1] - cuts[p], LANE) for p in range(len(cuts) - 1)]
+        n_copies = 2 * half * (len(cuts) - 1)
+    else:
+        grad_shapes = [(flat_rows, LANE)]
+        n_copies = 0
+    clip_spec = pl.BlockSpec((1, length, width), lambda i, c, m: (i, 0, 0))
+    fixed = lambda shape: pl.BlockSpec(shape, lambda i, c, m: (0, 0))
     grid_spec = pltpu.PrefetchScalarGridSpec(
-        num_scalar_prefetch=1,
+        num_scalar_prefetch=2,
         grid=(clips,),
         in_specs=[clip_spec, clip_spec, pl.BlockSpec(memory_space=pl.ANY),
                   fixed((8, width)), fixed((8, width)), fixed((8, hidden))],
-        out_specs=[clip_spec, clip_spec,
-                   pl.BlockSpec(memory_space=pl.ANY),
-                   fixed((8, width)), fixed((8, width)), fixed((8, hidden))],
+        out_specs=[clip_spec, clip_spec] + [pl.BlockSpec(memory_space=pl.ANY)] * len(grad_shapes)
+                  + [fixed((8, width)), fixed((8, width)), fixed((8, hidden))],
         scratch_shapes=[
             pltpu.VMEM(((length + 2 * PAD) * (width // LANE), LANE), F32),
             pltpu.VMEM((length, width), F32),
@@ -248,7 +273,7 @@
             pltpu.VMEM((2 * width * hidden // LANE, LANE), BF16),
             pltpu.VMEM((width, hidden), BF16),
             pltpu.VMEM((hidden, width), BF16),
-            pltpu.SemaphoreType.DMA((2,)),
+            pltpu.SemaphoreType.DMA((2 + n_copies,)),
         ],
     )
     flops = 12 * clips * length * width * hidden
@@ -260,7 +285,7 @@
         out_shape=[
             jax.ShapeDtypeStruct((clips, length, width), BF16),
             jax.ShapeDtypeStruct((clips, length, width), F32),
-            jax.ShapeDtypeStruct((flat_rows, LANE), F32),
+        ] + [jax.ShapeDtypeStruct(s, F32) for s in grad_shapes] + [
             jax.ShapeDtypeStruct((8, width), F32),
             jax.ShapeDtypeStruct((8, width), F32),
             jax.ShapeDtypeStruct((8, hidden), F32),
@@ -268,7 +293,7 @@
         compiler_params=pltpu.CompilerParams(
             dimension_semantics=("arbitrary",), vmem_limit_bytes=60 * 1024 * 1024),
         cost_estimate=cost,
-    )(counts, frames, cotangent, wrows, cw8, vec8, b1_8)
+    )(counts, my_bit, frames, cotangent, wrows, cw8, vec8, b1_8)
 
 
 def unpack(packed, width, hidden):
@@ -326,17 +351,18 @@
     return jnp.concatenate(parts, axis=1).reshape(devices * rows, LANES)
 
 
-def tree_reduce_scatter(full, orders, nbits):
+def row_cuts(rows, parts):
+    cuts = [rows * p // parts for p in range(parts + 1)]
+    if rows % 8 == 0:
+        cuts = [c // 8 * 8 for c in cuts]
+    return cuts
+
+
+def halve_steps(held, orders, nbits, first_step):
     me = lax.axis_index(AXES)
     devices = 1 << nbits
-    rows = full.shape[0] // devices
-    cuts = [rows * p // len(orders) for p in range(len(orders) + 1)]
-    if rows % 8 == 0:
-        cuts = [c // 8 * 8 for c in cuts]
-    shaped = full.reshape([2] * nbits + [rows, LANES])
-    held = [shaped[..., cuts[p]:cuts[p + 1], :] for p in range(len(orders))]
-    held_bits = [[nbits - 1 - a for a in range(nbits)] for _ in orders]
-    for step in range(nbits):
+    held_bits = [[b for b in range(nbits - 1, -1, -1) if b not in order[:first_step]] for order in orders]
+    for step in range(first_step, nbits):
         for p, order in enumerate(orders):
             bit = order[step]
             axis = held_bits[p].index(bit)
@@ -346,6 +372,15 @@
             held[p] = keep + lax.ppermute(send, AXES, swap_perm(devices, bit))
             held_bits[p].pop(axis)
     return jnp.concatenate(held, axis=0)
+
+
+def tree_reduce_scatter(full, orders, nbits):
+    devices = 1 << nbits
+    rows = full.shape[0] // devices
+    cuts = row_cuts(rows, len(orders))
+    shaped = full.reshape([2] * nbits + [rows, LANES])
+    held = [shaped[..., cuts[p]:cuts[p + 1], :] for p in range(len(orders))]
+    return halve_steps(held, orders, nbits, 0)
 
 
 def tree_all_sum(value, order, nbits):
@@ -382,9 +417,23 @@
     padded_rows = -(-shard_rows // 8) * 8
     aligned = padded_rows != shard_rows and (padded_rows - shard_rows) * (devices - 1) <= padded_rows
     block = padded_rows if aligned else shard_rows
-    block_out, input_grad, grad_full, _, _, _ = fused_block(
-        frames, counts, cotangent, packed_rows, cw8, vec8, b1_8, devices * block)
-    grad_block = tree_reduce_scatter(grad_full, split_orders(order), nbits)
+    orders = split_orders(order)
+    my_bit = (lax.axis_index(AXES) & 1).astype(jnp.int32).reshape(1)
+    if aligned and order[0] == 0 and all(o[0] == 0 for o in orders):
+        cuts = row_cuts(block, len(orders))
+        outs = fused_block(frames, counts, cotangent, packed_rows, cw8, vec8, b1_8, devices * block, my_bit,
+                           split=(block, tuple(cuts)))
+        block_out, input_grad = outs[0], outs[1]
+        held = []
+        for p in range(len(orders)):
+            halves = outs[2 + p]
+            got = lax.ppermute(halves[1], AXES, swap_perm(devices, 0))
+            held.append((halves[0] + got).reshape([2] * (nbits - 1) + [cuts[p + 1] - cuts[p], LANES]))
+        grad_block = halve_steps(held, orders, nbits, 1)
+    else:
+        block_out, input_grad, grad_full, _, _, _ = fused_block(
+            frames, counts, cotangent, packed_rows, cw8, vec8, b1_8, devices * block, my_bit)
+        grad_block = tree_reduce_scatter(grad_full, orders, nbits)
     if aligned:
         me = lax.axis_index(AXES)
         prev = lax.ppermute(grad_block, AXES, [(i, (i + 1) % devices) for i in range(devices)])

time: 255 us -> 261 us (1.024); the launches traced: 253 us -> 256 us
  starting transfers between devices: 53.6 us -> 64.3 us
  waiting for transfers between devices: 56.9 us -> 49.2 us
  local copies, waits for them, and re-layouts: 20.1 us -> 15.1 us
  Pallas kernels: 104 us -> 108 us
    ppermute x10, starting transfers between devices: 36.7 us -> 44.1 us  [the longest x8 43.5 us: halve_steps(): held[p] = keep + lax.ppermute(send, AXES, swap_perm(devices, bit))]
    pallas_call x1, Pallas kernels: 104 us -> 108 us  [fused_block(): pl.pallas_call(kernel, grid_spec=grid_spec, out_shape=[jax.ShapeDtypeStru...]
    ppermute x10, waiting for transfers between devices: 27.1 us -> 23 us  [the longest x8 21.6 us: halve_steps(): held[p] = keep + lax.ppermute(send, AXES, swap_perm(devices, bit))]
    ppermute x5, waiting for transfers between devices: 14.8 us -> 11.2 us  [tree_all_sum(): value = value + lax.ppermute(value, AXES, swap_perm(devices, bit))]
    ppermute x5, starting transfers between devices: 2.13 us -> 5.37 us  [tree_all_sum(): value = value + lax.ppermute(value, AXES, swap_perm(devices, bit))]
    unnamed x30 -> x18, local copies, waits for them, and re-layouts: 4.43 us -> 1.51 us
  transfers between devices with their start and end apart: 26 -> 26, of which waited for: 21 -> 22; matrix products, arithmetic and copies ran while one was open for 7% -> 7% of each run, Pallas kernels for 0% -> 0%
where the time goes in v2:
time: 261 us; the launch traced here: 256 us
  Pallas kernels  108 us (41%)
  starting transfers between devices  64.3 us (25%)
  waiting for transfers between devices  49.2 us (19%)
  other arithmetic  16.2 us (6%)
  local copies, waits for them, and re-layouts  15.1 us (6%)
  between operations  2.88 us (1%)
    pallas_call x1, Pallas kernels, fused_block(): pl.pallas_call(kernel, grid_spec=grid_spec, out_shape=[jax.ShapeDtypeStru...  108 us
    ppermute x8, starting transfers between devices, halve_steps(): held[p] = keep + lax.ppermute(send, AXES, swap_perm(devices, bit))  43.5 us
    ppermute x8, waiting for transfers between devices, halve_steps(): held[p] = keep + lax.ppermute(send, AXES, swap_perm(devices, bit))  21.6 us
    ppermute x10, waiting for transfers between devices, tree_all_gather(): other = lax.ppermute(held[p], AXES, swap_perm(devices, bit))  15 us
    ppermute x10, starting transfers between devices, tree_all_gather(): other = lax.ppermute(held[p], AXES, swap_perm(devices, bit))  14.8 us
    ppermute x5, waiting for transfers between devices, tree_all_sum(): value = value + lax.ppermute(value, AXES, swap_perm(devices, bit))  11.2 us
    ppermute x5, starting transfers between devices, tree_all_sum(): value = value + lax.ppermute(value, AXES, swap_perm(devices, bit))  5.37 us
  transfers between devices with their start and end apart: 26, of which 22 were waited for; matrix products, arithmetic and copies ran while one was open for 7% of the time, Pallas kernels for 0%

profile of v2, /device:TPU:0, one launch (start us, length us, event | category | flops | bytes accessed | tf_op | source)
XLA Modules:
  0.0 255.9 jit_solution(769576180142320896)
XLA Ops:
  1.6 4.1 %collective-permute-start = (bf16[1,1,1,1,1,192,128]{6,5,4,3,2,1,0:T(8,128)(2,1)S(1)}, bf16[1,1,1,1,1,192,128]{6,5,4,3,2,1,0:T(8,128)(2,1)S(1)}, u32[]{:S(2)}, u32[]{:S(2)}) collective-permute-start(bf16[1,1,1,1,1,192,128]{6,5,4,3,2,1,0:T(8,128)(2,1)S(1)} %slice_bitcast_fusion.3), channel_id=1, source_target_pairs={{0,4},{1,5},{2,6},{3,7},{4,0},{5,1},{6,2},{7,3},{8,12},{9,13},{10,... | collective-permute-start | bytes 147464 | tf_op jit(solution)/shard_map/ppermute | solution.py:346
  5.8 2.5 collective-permute-done
  8.4 2.2 collective-permute-start.1
  17.3 2.5 collective-permute-done.2
  23.0 1.7 collective-permute-start.8
  24.7 5.2 %collective-permute-done.3 = bf16[2,1,2,2,1,192,128]{6,5,4,3,2,1,0:T(8,128)(2,1)S(1)} collective-permute-done((bf16[2,1,2,2,1,192,128]{6,5,4,3,2,1,0:T(8,128)(2,1)S(1)}, bf16[2,1,2,2,1,192,128]{6,5,4,3,2,1,0:T(8,128)(2,1)S(1)}, u32[]{:S(2)}, u32[]{:S(2)}) %collective-permute-start.3) | collective-permute-done | bytes 393248 | tf_op jit(solution)/shard_map/ppermute | solution.py:346
  39.1 2.7 %reshape.138.wrows_hbm = bf16[12352,128]{1,0:T(8,128)(2,1)} reshape(bf16[32,386,128]{2,1,0:T(8,128)(2,1)S(1)} %copy.31) | data formatting | bytes 6324224 | tf_op jit(solution)/shard_map/reshape | solution.py:351
  45.9 108.2 %shard_map.134 = (bf16[8,1024,512]{2,1,0:T(8,128)(2,1)}, f32[8,1024,512]{2,1,0:T(8,128)}, f32[2,16,192,128]{3,2,1,0:T(8,128)}, f32[2,16,200,128]{3,2,1,0:T(8,128...) custom-call(s32[8]{0:T(128)} %counts_ref.1, s32[1]{0:T(128)} %bitcast.bit_ref, ...), custom_call_target="tpu_custom_call" | custom-call | flops 77309411328 | bytes 46137344 | tf_op jit(solution)/shard_map/pallas_call | solution.py:282
  159.3 2.2 bitcast_add_fusion.1
  162.4 1.6 bitcast_add_fusion
  165.0 10.9 %collective-permute-start.16 = (f32[2,2,2,200,128]{4,3,2,1,0:T(8,128)}, f32[2,2,2,200,128]{4,3,2,1,0:T(8,128)}, u32[]{:S(2)}, u32[]{:S(2)}) collective-permute-start(f32[2,2,2,200,128]{4,3,2,1,0:T(8,128)} %dynamic-slice_bitcast_fusion), channel_id=1, source_target_pairs={{0,16},{1,17},{2,18},{3,19},{4,20},{5,21},{6,22},{7,23},{8,24},{9,... | collective-permute-start | bytes 2457608 | tf_op jit(solution)/shard_map/ppermute | solution.py:372
  175.9 6.4 %collective-permute-done.11 = f32[2,2,2,192,128]{4,3,2,1,0:T(8,128)} collective-permute-done((f32[2,2,2,192,128]{4,3,2,1,0:T(8,128)}, f32[2,2,2,192,128]{4,3,2,1,0:T(8,128)}, u32[]{:S(2)}, u32[]{:S(2)}) %collective-permute-start.11) | collective-permute-done | bytes 786464 | tf_op jit(solution)/shard_map/ppermute | solution.py:372
  184.4 9.4 %collective-permute-start.12 = (f32[2,2,192,128]{3,2,1,0:T(8,128)}, f32[2,2,192,128]{3,2,1,0:T(8,128)}, u32[]{:S(2)}, u32[]{:S(2)}) collective-permute-start(f32[2,2,192,128]{3,2,1,0:T(8,128)} %dynamic-slice_bitcast_fusion.3), channel_id=1, source_target_pairs={{0,16},{1,17},{2,18},{3,19},{4,20},{5,21},{6,22},{7,23},{8,24},{9,... | collective-permute-start | bytes 1179656 | tf_op jit(solution)/shard_map/ppermute | solution.py:372
  196.7 6.2 %collective-permute-done.12 = f32[2,2,192,128]{3,2,1,0:T(8,128)} collective-permute-done((f32[2,2,192,128]{3,2,1,0:T(8,128)}, f32[2,2,192,128]{3,2,1,0:T(8,128)}, u32[]{:S(2)}, u32[]{:S(2)}) %collective-permute-start.12) | collective-permute-done | bytes 393248 | tf_op jit(solution)/shard_map/ppermute | solution.py:372
  204.1 2.2 collective-permute-start.13
  207.9 4.2 %collective-permute-done.13 = f32[2,192,128]{2,1,0:T(8,128)S(1)} collective-permute-done((f32[2,192,128]{2,1,0:T(8,128)S(1)}, f32[2,192,128]{2,1,0:T(8,128)S(1)}, u32[]{:S(2)}, u32[]{:S(2)}) %collective-permute-start.13) | collective-permute-done | bytes 196640 | tf_op jit(solution)/shard_map/ppermute | solution.py:372
  212.2 15.2 %collective-permute-start.14 = (f32[192,128]{1,0:T(8,128)S(1)}, f32[192,128]{1,0:T(8,128)S(1)}, u32[]{:S(2)}, u32[]{:S(2)}) collective-permute-start(f32[192,128]{1,0:T(8,128)S(1)} %dynamic-slice_bitcast_fusion.7), channel_id=1, source_target_pairs={{0,4},{1,5},{2,6},{3,7},{4,0},{5,1},{6,2},{7,3},{8,12},{9,13},{10,... | collective-permute-start | bytes 294920 | tf_op jit(solution)/shard_map/ppermute | solution.py:372
  227.4 3.8 %collective-permute-start.19 = (f32[200,128]{1,0:T(8,128)S(1)}, f32[200,128]{1,0:T(8,128)S(1)}, u32[]{:S(2)}, u32[]{:S(2)}) collective-permute-start(f32[200,128]{1,0:T(8,128)S(1)} %dynamic-slice_bitcast_fusion.6), channel_id=1, source_target_pairs={{0,4},{1,5},{2,6},{3,7},{4,0},{5,1},{6,2},{7,3},{8,12},{9,13},{10,... | collective-permute-start | bytes 307208 | tf_op jit(solution)/shard_map/ppermute | solution.py:372
  232.8 2.3 collective-permute-done.19
  235.1 2.0 collective-permute-start.20
  237.2 2.5 collective-permute-done.20
  240.8 2.5 collective-permute-done.21
  244.1 2.8 %collective-permute-done.22 = f32[8,128]{1,0:T(8,128)S(1)} collective-permute-done((f32[8,128]{1,0:T(8,128)S(1)}, f32[8,128]{1,0:T(8,128)S(1)}, u32[]{:S(2)}, u32[]{:S(2)}) %collective-permute-start.22) | collective-permute-done | bytes 4128 | tf_op jit(solution)/shard_map/ppermute | solution.py:389
  248.4 2.1 collective-permute-done.23
  (116 shorter events, 47.4 us)
Async XLA Ops:
  1.6 6.7 %collective-permute-start = (bf16[1,1,1,1,1,192,128]{6,5,4,3,2,1,0:T(8,128)(2,1)S(1)}, bf16[1,1,1,1,1,192,128]{6,5,4,3,2,1,0:T(8,128)(2,1)S(1)}, u32[]{:S(2)}, u32[]{:S(2)}) collective-permute-start(bf16[1,1,1,1,1,192,128]{6,5,4,3,2,1,0:T(8,128)(2,1)S(1)} %slice_bitcast_fusion.3), channel_id=1, source_target_pairs={{0,4},{1,5},{2,6},{3,7},{4,0},{5,1},{6,2},{7,3},{8,12},{9,13},{10,... | collective-permute-start | bytes 147464 | tf_op jit(solution)/shard_map/ppermute | solution.py:346
  5.7 5.2 %collective-permute-start.5 = (bf16[1,1,1,1,1,194,128]{6,5,4,3,2,1,0:T(8,128)(2,1)S(1)}, bf16[1,1,1,1,1,194,128]{6,5,4,3,2,1,0:T(8,128)(2,1)S(1)}, u32[]{:S(2)}, u32[]{:S(2)}) collective-permute-start(bf16[1,1,1,1,1,194,128]{6,5,4,3,2,1,0:T(8,128)(2,1)S(1)} %slice_bitcast_fusion.2), channel_id=1, source_target_pairs={{0,4},{1,5},{2,6},{3,7},{4,0},{5,1},{6,2},{7,3},{8,12},{9,13},{10,... | collective-permute-start | bytes 149000 | tf_op jit(solution)/shard_map/ppermute | solution.py:346
  8.4 5.6 %collective-permute-start.1 = (bf16[1,1,2,1,1,192,128]{6,5,4,3,2,1,0:T(8,128)(2,1)S(1)}, bf16[1,1,2,1,1,192,128]{6,5,4,3,2,1,0:T(8,128)(2,1)S(1)}, u32[]{:S(2)}, u32[]{:S(2)}) collective-permute-start(bf16[1,1,2,1,1,192,128]{6,5,4,3,2,1,0:T(8,128)(2,1)S(1)} %pad_maximum_fusion.11), channel_id=1, source_target_pairs={{0,2},{1,3},{2,0},{3,1},{4,6},{5,7},{6,4},{7,5},{8,10},{9,11},{10,... | collective-permute-start | bytes 294920 | tf_op jit(solution)/shard_map/ppermute | solution.py:346
  10.9 4.7 %collective-permute-start.6 = (bf16[1,1,2,1,1,194,128]{6,5,4,3,2,1,0:T(8,128)(2,1)S(1)}, bf16[1,1,2,1,1,194,128]{6,5,4,3,2,1,0:T(8,128)(2,1)S(1)}, u32[]{:S(2)}, u32[]{:S(2)}) collective-permute-start(bf16[1,1,2,1,1,194,128]{6,5,4,3,2,1,0:T(8,128)(2,1)S(1)} %pad_maximum_fusion.10), channel_id=1, source_target_pairs={{0,2},{1,3},{2,0},{3,1},{4,6},{5,7},{6,4},{7,5},{8,10},{9,11},{10,... | collective-permute-start | bytes 297992 | tf_op jit(solution)/shard_map/ppermute | solution.py:346
  14.0 5.7 %collective-permute-start.2 = (bf16[1,1,2,2,1,192,128]{6,5,4,3,2,1,0:T(8,128)(2,1)S(1)}, bf16[1,1,2,2,1,192,128]{6,5,4,3,2,1,0:T(8,128)(2,1)S(1)}, u32[]{:S(2)}, u32[]{:S(2)}) collective-permute-start(bf16[1,1,2,2,1,192,128]{6,5,4,3,2,1,0:T(8,128)(2,1)S(1)} %pad_maximum_fusion.9), channel_id=1, source_target_pairs={{0,16},{1,17},{2,18},{3,19},{4,20},{5,21},{6,22},{7,23},{8,24},{9,... | collective-permute-start | bytes 589832 | tf_op jit(solution)/shard_map/ppermute | solution.py:346
  15.7 7.2 %collective-permute-start.7 = (bf16[1,1,2,2,1,194,128]{6,5,4,3,2,1,0:T(8,128)(2,1)S(1)}, bf16[1,1,2,2,1,194,128]{6,5,4,3,2,1,0:T(8,128)(2,1)S(1)}, u32[]{:S(2)}, u32[]{:S(2)}) collective-permute-start(bf16[1,1,2,2,1,194,128]{6,5,4,3,2,1,0:T(8,128)(2,1)S(1)} %pad_maximum_fusion.7), channel_id=1, source_target_pairs={{0,8},{1,9},{2,10},{3,11},{4,12},{5,13},{6,14},{7,15},{8,0},{9,1},... | collective-permute-start | bytes 595976 | tf_op jit(solution)/shard_map/ppermute | solution.py:346
  19.8 10.2 %collective-permute-start.3 = (bf16[2,1,2,2,1,192,128]{6,5,4,3,2,1,0:T(8,128)(2,1)S(1)}, bf16[2,1,2,2,1,192,128]{6,5,4,3,2,1,0:T(8,128)(2,1)S(1)}, u32[]{:S(2)}, u32[]{:S(2)}) collective-permute-start(bf16[2,1,2,2,1,192,128]{6,5,4,3,2,1,0:T(8,128)(2,1)S(1)} %pad_maximum_fusion.6), channel_id=1, source_target_pairs={{0,8},{1,9},{2,10},{3,11},{4,12},{5,13},{6,14},{7,15},{8,0},{9,1},... | collective-permute-start | bytes 1179656 | tf_op jit(solution)/shard_map/ppermute | solution.py:346
  23.0 8.0 %collective-permute-start.8 = (bf16[1,2,2,2,1,194,128]{6,5,4,3,2,1,0:T(8,128)(2,1)S(1)}, bf16[1,2,2,2,1,194,128]{6,5,4,3,2,1,0:T(8,128)(2,1)S(1)}, u32[]{:S(2)}, u32[]{:S(2)}) collective-permute-start(bf16[1,2,2,2,1,194,128]{6,5,4,3,2,1,0:T(8,128)(2,1)S(1)} %pad_maximum_fusion.5), channel_id=1, source_target_pairs={{0,16},{1,17},{2,18},{3,19},{4,20},{5,21},{6,22},{7,23},{8,24},{9,... | collective-permute-start | bytes 1191944 | tf_op jit(solution)/shard_map/ppermute | solution.py:346
  31.8 4.2 %collective-permute-start.9 = (bf16[2,2,2,2,1,194,128]{6,3,5,4,2,1,0:T(2,128)(2,1)S(1)}, bf16[2,2,2,2,1,194,128]{6,3,5,4,2,1,0:T(2,128)(2,1)S(1)}, u32[]{:S(2)}, u32[]{:S(2)}) collective-permute-start(bf16[2,2,2,2,1,194,128]{6,3,5,4,2,1,0:T(2,128)(2,1)S(1)} %copy.26), channel_id=1, source_target_pairs={{0,1},{1,0},{2,3},{3,2},{4,5},{5,4},{6,7},{7,6},{8,9},{9,8},{10,11... | collective-permute-start | bytes 2383880 | tf_op jit(solution)/shard_map/ppermute | solution.py:346
  155.6 3.6 %collective-permute-start.10 = (f32[16,192,128]{2,1,0:T(8,128)S(1)}, f32[16,192,128]{2,1,0:T(8,128)}, u32[]{:S(2)}, u32[]{:S(2)}) collective-permute-start(f32[16,192,128]{2,1,0:T(8,128)S(1)} %slice_bitcast_fusion.1), channel_id=1, source_target_pairs={{0,1},{1,0},{2,3},{3,2},{4,5},{5,4},{6,7},{7,6},{8,9},{9,8},{10,11... | collective-permute-start | bytes 4718600 | tf_op jit(solution)/shard_map/ppermute | solution.py:430
  157.3 5.1 %collective-permute-start.15 = (f32[16,200,128]{2,1,0:T(8,128)S(1)}, f32[16,200,128]{2,1,0:T(8,128)}, u32[]{:S(2)}, u32[]{:S(2)}) collective-permute-start(f32[16,200,128]{2,1,0:T(8,128)S(1)} %slice_bitcast_fusion), channel_id=1, source_target_pairs={{0,1},{1,0},{2,3},{3,2},{4,5},{5,4},{6,7},{7,6},{8,9},{9,8},{10,11... | collective-permute-start | bytes 4915208 | tf_op jit(solution)/shard_map/ppermute | solution.py:430
  162.4 19.9 %collective-permute-start.11 = (f32[2,2,2,192,128]{4,3,2,1,0:T(8,128)}, f32[2,2,2,192,128]{4,3,2,1,0:T(8,128)}, u32[]{:S(2)}, u32[]{:S(2)}) collective-permute-start(f32[2,2,2,192,128]{4,3,2,1,0:T(8,128)} %dynamic-slice_bitcast_fusion.1), channel_id=1, source_target_pairs={{0,8},{1,9},{2,10},{3,11},{4,12},{5,13},{6,14},{7,15},{8,0},{9,1},... | collective-permute-start | bytes 2359304 | tf_op jit(solution)/shard_map/ppermute | solution.py:372
  165.0 29.7 %collective-permute-start.16 = (f32[2,2,2,200,128]{4,3,2,1,0:T(8,128)}, f32[2,2,2,200,128]{4,3,2,1,0:T(8,128)}, u32[]{:S(2)}, u32[]{:S(2)}) collective-permute-start(f32[2,2,2,200,128]{4,3,2,1,0:T(8,128)} %dynamic-slice_bitcast_fusion), channel_id=1, source_target_pairs={{0,16},{1,17},{2,18},{3,19},{4,20},{5,21},{6,22},{7,23},{8,24},{9,... | collective-permute-start | bytes 2457608 | tf_op jit(solution)/shard_map/ppermute | solution.py:372
  184.4 18.5 %collective-permute-start.12 = (f32[2,2,192,128]{3,2,1,0:T(8,128)}, f32[2,2,192,128]{3,2,1,0:T(8,128)}, u32[]{:S(2)}, u32[]{:S(2)}) collective-permute-start(f32[2,2,192,128]{3,2,1,0:T(8,128)} %dynamic-slice_bitcast_fusion.3), channel_id=1, source_target_pairs={{0,16},{1,17},{2,18},{3,19},{4,20},{5,21},{6,22},{7,23},{8,24},{9,... | collective-permute-start | bytes 1179656 | tf_op jit(solution)/shard_map/ppermute | solution.py:372
  196.0 10.5 %collective-permute-start.17 = (f32[2,2,200,128]{3,2,1,0:T(8,128)S(1)}, f32[2,2,200,128]{3,2,1,0:T(8,128)S(1)}, u32[]{:S(2)}, u32[]{:S(2)}) collective-permute-start(f32[2,2,200,128]{3,2,1,0:T(8,128)S(1)} %dynamic-slice_bitcast_fusion.2), channel_id=1, source_target_pairs={{0,8},{1,9},{2,10},{3,11},{4,12},{5,13},{6,14},{7,15},{8,0},{9,1},... | collective-permute-start | bytes 1228808 | tf_op jit(solution)/shard_map/ppermute | solution.py:372
  204.1 8.0 %collective-permute-start.13 = (f32[2,192,128]{2,1,0:T(8,128)S(1)}, f32[2,192,128]{2,1,0:T(8,128)S(1)}, u32[]{:S(2)}, u32[]{:S(2)}) collective-permute-start(f32[2,192,128]{2,1,0:T(8,128)S(1)} %dynamic-slice_bitcast_fusion.5), channel_id=1, source_target_pairs={{0,2},{1,3},{2,0},{3,1},{4,6},{5,7},{6,4},{7,5},{8,10},{9,11},{10,... | collective-permute-start | bytes 589832 | tf_op jit(solution)/shard_map/ppermute | solution.py:372
  206.6 20.8 %collective-permute-start.18 = (f32[2,200,128]{2,1,0:T(8,128)S(1)}, f32[2,200,128]{2,1,0:T(8,128)S(1)}, u32[]{:S(2)}, u32[]{:S(2)}) collective-permute-start(f32[2,200,128]{2,1,0:T(8,128)S(1)} %dynamic-slice_bitcast_fusion.4), channel_id=1, source_target_pairs={{0,2},{1,3},{2,0},{3,1},{4,6},{5,7},{6,4},{7,5},{8,10},{9,11},{10,... | collective-permute-start | bytes 614408 | tf_op jit(solution)/shard_map/ppermute | solution.py:372
  212.2 20.6 %collective-permute-start.14 = (f32[192,128]{1,0:T(8,128)S(1)}, f32[192,128]{1,0:T(8,128)S(1)}, u32[]{:S(2)}, u32[]{:S(2)}) collective-permute-start(f32[192,128]{1,0:T(8,128)S(1)} %dynamic-slice_bitcast_fusion.7), channel_id=1, source_target_pairs={{0,4},{1,5},{2,6},{3,7},{4,0},{5,1},{6,2},{7,3},{8,12},{9,13},{10,... | collective-permute-start | bytes 294920 | tf_op jit(solution)/shard_map/ppermute | solution.py:372
  227.4 7.6 %collective-permute-start.19 = (f32[200,128]{1,0:T(8,128)S(1)}, f32[200,128]{1,0:T(8,128)S(1)}, u32[]{:S(2)}, u32[]{:S(2)}) collective-permute-start(f32[200,128]{1,0:T(8,128)S(1)} %dynamic-slice_bitcast_fusion.6), channel_id=1, source_target_pairs={{0,4},{1,5},{2,6},{3,7},{4,0},{5,1},{6,2},{7,3},{8,12},{9,13},{10,... | collective-permute-start | bytes 307208 | tf_op jit(solution)/shard_map/ppermute | solution.py:372
  235.1 4.6 %collective-permute-start.20 = (f32[8,128]{1,0:T(8,128)S(1)}, f32[8,128]{1,0:T(8,128)S(1)}, u32[]{:S(2)}, u32[]{:S(2)}) collective-permute-start(f32[8,128]{1,0:T(8,128)S(1)} %broadcast_in_dim.2), channel_id=1, source_target_pairs={{0,4},{1,5},{2,6},{3,7},{4,0},{5,1},{6,2},{7,3},{8,12},{9,13},{10,... | collective-permute-start | bytes 12296 | tf_op jit(solution)/shard_map/ppermute | solution.py:389
  239.7 3.6 %collective-permute-start.21 = (f32[8,128]{1,0:T(8,128)S(1)}, f32[8,128]{1,0:T(8,128)S(1)}, u32[]{:S(2)}, u32[]{:S(2)}) collective-permute-start(f32[8,128]{1,0:T(8,128)S(1)} %broadcast_add_fusion), channel_id=1, source_target_pairs={{0,2},{1,3},{2,0},{3,1},{4,6},{5,7},{6,4},{7,5},{8,10},{9,11},{10,... | collective-permute-start | bytes 12296 | tf_op jit(solution)/shard_map/ppermute | solution.py:389
  240.8 12.3 %collective-permute-start.25 = (f32[392,128]{1,0:T(8,128)S(1)}, f32[392,128]{1,0:T(8,128)S(1)}, u32[]{:S(2)}, u32[]{:S(2)}) collective-permute-start(f32[392,128]{1,0:T(8,128)S(1)} %get-tuple-element.63), channel_id=1, source_target_pairs={{0,1},{1,2},{2,3},{3,4},{4,5},{5,6},{6,7},{7,8},{8,9},{9,10},{10,1... | collective-permute-start | bytes 602120 | tf_op jit(solution)/shard_map/ppermute | solution.py:439
  243.3 3.6 %collective-permute-start.22 = (f32[8,128]{1,0:T(8,128)S(1)}, f32[8,128]{1,0:T(8,128)S(1)}, u32[]{:S(2)}, u32[]{:S(2)}) collective-permute-start(f32[8,128]{1,0:T(8,128)S(1)} %fusion.5), channel_id=1, source_target_pairs={{0,16},{1,17},{2,18},{3,19},{4,20},{5,21},{6,22},{7,23},{8,24},{9,... | collective-permute-start | bytes 12296 | tf_op jit(solution)/shard_map/ppermute | solution.py:389
  246.9 3.6 %collective-permute-start.23 = (f32[8,128]{1,0:T(8,128)S(1)}, f32[8,128]{1,0:T(8,128)S(1)}, u32[]{:S(2)}, u32[]{:S(2)}) collective-permute-start(f32[8,128]{1,0:T(8,128)S(1)} %add.151), channel_id=1, source_target_pairs={{0,8},{1,9},{2,10},{3,11},{4,12},{5,13},{6,14},{7,15},{8,0},{9,1},... | collective-permute-start | bytes 12296 | tf_op jit(solution)/shard_map/ppermute | solution.py:389
  (9 other events, 169.7 us)
